TPU v7x, 512 devices: a whole 4x4x16 slice. The times are simulated.
512 devices in a mesh: kv: 8 (over y, core), pages: 64 (over x, z).
Axes of the slice: x: 4, y: 4, z: 16, core: 2. Of those that a mesh axis runs over, the one named last changes fastest.
Arguments:
- tokens: int32 [2, 64], replicated, may hold values from 0 to 31999
- prompt_len: int32 [8], replicated, may hold values from 193 to 8192, as said below
- page_table: int32 [8, 64], replicated, may hold values from -1 to 511, as said below
- parents: int32 [2, 64], replicated, may hold values from 0 to 63, as said below
- embedding: bfloat16 [32000, 7168], P('kv', 'pages'), may hold values from -6 to 6
- norm_gain: bfloat16 [7168], P('pages'), may hold values from 0.099609375 to 1.8984375
- w_qkv: bfloat16 [7168, 9216], P('pages', 'kv'), may hold values from -0.0625 to 0.0625
- w_out: bfloat16 [7168, 7168], P('kv', 'pages'), may hold values from -0.8984375 to 0.8984375
- history: bfloat16 [2, 64, 13, 1024], P(None, None, None, 'kv'), may hold values from -6 to 6
- kv_pool: bfloat16 [2, 512, 128, 1024], P(None, 'pages', None, 'kv'), may hold values from -400 to 400
Outputs:
- hidden: bfloat16 [2, 64, 7168], P(None, None, 'pages')
- history_out: bfloat16 [2, 64, 15, 1024], P(None, None, None, 'kv')
Inputs may be any that keep to these rules, and one draw needn't show every extreme that they name: `prompt_len`: each prompt is either long, within 512 tokens below 8192, or short, within 64 tokens below 256; some group's prompt has exactly 8192 tokens. For j below prompt_len[g] / 128 rounded up, page_table[g, j] is the slot holding tokens j * 128 to j * 128 + 127 of group g's prompt; no slot is named twice; all other entries are -1. parents[t, b] is a beam of b's group; at the first step the first and the last beam of every group continue their own history.
All inputs are finite; a program needn't handle non-finite values.
Results may differ from a plain program's by a relative error of at most 0.015.
The roundings to bfloat16 on the way count: a program that leaves them out, or rounds other values in their place, can miss the bound.
Values may be sent and summed in bfloat16 or wider, within the bound.
No kernel may reach another device: no remote copies, remote signals or barrier semaphores. Data moves between devices by JAX's collectives and lax.ppermute only.
A program may use at most 128 MiB of HBM per device.

v0:
```python
import jax
import jax.numpy as jnp
from jax import lax
from jax.sharding import PartitionSpec as P

D = 7168
KV_HEADS = 8
HEAD_DIM = 128
GROUPS = 8
BEAMS = 8
PRIOR = 13
PAGE = 128
PER_KV = 7
HISTORY = 15
MAX_PAGES = 64


THETA = 5000000.0
EPSILON = 1e-05
NEGATIVE = -1e30


def merged(part, axis, combine):
    gathered = jax.tree.map(lambda a: lax.all_gather(a, axis), part)

    def take(source):
        return jax.tree.map(lambda a: lax.dynamic_index_in_dim(a, source, 0, False), gathered)

    return lax.fori_loop(
        1, lax.axis_size(axis), lambda source, state: combine(state, take(source)), take(0)
    )


def rotate(values, positions):
    half_dim = HEAD_DIM // 2
    frequency = THETA ** (-(2.0 * jnp.arange(half_dim, dtype=jnp.float32)) / HEAD_DIM)
    angles = positions.astype(jnp.float32)[:, None] * frequency[None, :]
    cosine = jnp.cos(angles)[:, None, None, :]
    sine_part = jnp.sin(angles)[:, None, None, :]
    lower_part = values[..., :half_dim]
    upper_part = values[..., half_dim:]
    return jnp.concatenate(
        [
            lower_part * cosine - upper_part * sine_part,
            upper_part * cosine + lower_part * sine_part,
        ],
        axis=-1,
    )


def finish_rows(summed, norm_sums, row_ids, prompt_len, num_seqs, local_heads):
    inverse_rms = lax.rsqrt(norm_sums / D + EPSILON)
    projected = (summed * inverse_rms[:, None]).reshape(-1, local_heads, PER_KV + 2, HEAD_DIM)
    positions = jnp.take(prompt_len, row_ids % num_seqs // BEAMS) + PRIOR + row_ids // num_seqs
    turned = rotate(projected[:, :, : PER_KV + 1], positions)
    return jnp.concatenate([turned, projected[:, :, PER_KV + 1 :]], axis=2).astype(jnp.bfloat16)


def combine(earlier, later):
    peak = jnp.maximum(earlier[0], later[0])
    weight_one = jnp.exp(earlier[0] - peak)
    weight_two = jnp.exp(later[0] - peak)
    return (
        peak,
        earlier[1] * weight_one + later[1] * weight_two,
        earlier[2] * weight_one[:, None] + later[2] * weight_two[:, None],
    )


def per_device(
    tokens, prompt_len, page_table, parents, embedding, norm_gain, w_qkv, w_out, history, kv_pool
):
    num_steps, num_seqs = tokens.shape
    row_count = num_steps * num_seqs
    local_heads = KV_HEADS // lax.axis_size("kv")
    kv_width = local_heads * HEAD_DIM
    inv_root = 1.0 / jnp.sqrt(jnp.float32(HEAD_DIM))
    vocab_local = embedding.shape[0]
    local_ids = tokens.reshape(-1) - lax.axis_index("kv") * vocab_local
    inside = (local_ids >= 0) & (local_ids < vocab_local)
    picked = jnp.take(embedding, jnp.clip(local_ids, 0, vocab_local - 1), axis=0)
    found = jnp.where(inside[:, None], picked.astype(jnp.float32), 0.0)
    embedded = lax.psum(found.astype(jnp.bfloat16), "kv")
    widened = embedded.astype(jnp.float32)
    squares = jnp.sum(widened * widened, axis=1)
    normed = (widened * norm_gain.astype(jnp.float32)).astype(jnp.bfloat16)
    partial_value = jnp.dot(normed, w_qkv, preferred_element_type=jnp.float32)
    summed, norm_sums = lax.psum((partial_value, squares), "pages")
    projected = finish_rows(
        summed, norm_sums, jnp.arange(row_count, dtype=jnp.int32), prompt_len, num_seqs, local_heads
    )
    queries = projected[:, :, :PER_KV]
    fresh_kv = jnp.stack([projected[:, :, PER_KV], projected[:, :, PER_KV + 1]]).reshape(
        2, num_steps, num_seqs, kv_width
    )
    buffer = jnp.concatenate(
        [history, jnp.zeros((2, num_seqs, num_steps, kv_width), jnp.bfloat16)], axis=2
    )
    snapshots = []
    for step_index in range(num_steps):
        buffer = jnp.take(buffer, parents[step_index], axis=1)
        buffer = buffer.at[:, :, PRIOR + step_index].set(fresh_kv[:, step_index])
        snapshots.append(buffer)
    stacked = jnp.stack(snapshots)
    tail_keys = stacked[:, 0].reshape(num_steps, num_seqs, HISTORY, local_heads, HEAD_DIM)
    tail_vals = stacked[:, 1].reshape(num_steps, num_seqs, HISTORY, local_heads, HEAD_DIM)
    step_query = queries.reshape(num_steps, num_seqs, local_heads, PER_KV, HEAD_DIM)
    tail_len = PRIOR + 1 + jnp.arange(num_steps, dtype=jnp.int32)
    tail_valid = (jnp.arange(HISTORY, dtype=jnp.int32)[None, :] < tail_len[:, None])[
        :, None, None, None, :
    ]
    tail_scores = (
        jnp.einsum("tbkhd,tblkd->tbkhl", step_query, tail_keys, preferred_element_type=jnp.float32)
        * inv_root
    )
    tail_scores = jnp.where(tail_valid, tail_scores, NEGATIVE)
    tail_peak = jnp.max(tail_scores, axis=-1)
    tail_exp = jnp.where(tail_valid, jnp.exp(tail_scores - tail_peak[..., None]), 0.0)
    tail_total = jnp.sum(tail_exp, axis=-1)
    tail_acc = jnp.einsum(
        "tbkhl,tblkd->tbkhd",
        tail_exp.astype(jnp.bfloat16),
        tail_vals,
        preferred_element_type=jnp.float32,
    )
    tail_part = (tail_peak.reshape(-1), tail_total.reshape(-1), tail_acc.reshape(-1, HEAD_DIM))
    slot_rows = kv_pool.shape[1]
    slot_ids = lax.axis_index("pages") * slot_rows + jnp.arange(slot_rows, dtype=jnp.int32)
    matches = page_table[:, :, None] == slot_ids[None, None, :]
    slot_used = jnp.any(matches, axis=(0, 1))
    owner_group = jnp.sum(
        jnp.where(matches, jnp.arange(GROUPS, dtype=jnp.int32)[:, None, None], 0), axis=(0, 1)
    )
    page_number = jnp.sum(
        jnp.where(matches, jnp.arange(MAX_PAGES, dtype=jnp.int32)[None, :, None], 0), axis=(0, 1)
    )
    length = jnp.take(prompt_len, owner_group)
    live_tok = slot_used[:, None] & (
        page_number[:, None] * PAGE + jnp.arange(PAGE, dtype=jnp.int32)[None, :] < length[:, None]
    )
    live_full = live_tok[None, :, None, :]
    grouped = queries.reshape(num_steps, GROUPS, BEAMS, local_heads, PER_KV, HEAD_DIM)
    chosen = jnp.take(grouped, owner_group, axis=1)
    query_rows = num_steps * BEAMS * PER_KV
    chosen = jnp.transpose(chosen, (3, 1, 0, 2, 4, 5)).reshape(
        local_heads, slot_rows, query_rows, HEAD_DIM
    )
    page_keys = jnp.transpose(
        kv_pool[0].reshape(slot_rows, PAGE, local_heads, HEAD_DIM), (2, 0, 1, 3)
    )
    page_vals = jnp.transpose(
        kv_pool[1].reshape(slot_rows, PAGE, local_heads, HEAD_DIM), (2, 0, 1, 3)
    )
    scores = (
        jnp.einsum("ksqd,kspd->ksqp", chosen, page_keys, preferred_element_type=jnp.float32)
        * inv_root
    )
    scores = jnp.where(live_full, scores, NEGATIVE)
    slot_peak = jnp.max(scores, axis=-1)
    slot_exp = jnp.where(live_full, jnp.exp(scores - slot_peak[..., None]), 0.0)
    slot_total = jnp.sum(slot_exp, axis=-1)
    slot_acc = jnp.einsum(
        "ksqp,kspd->ksqd",
        slot_exp.astype(jnp.bfloat16),
        page_vals,
        preferred_element_type=jnp.float32,
    )
    member = (owner_group[:, None] == jnp.arange(GROUPS, dtype=jnp.int32)[None, :]) & slot_used[
        :, None
    ]
    spread = jnp.where(member[None, :, :, None], slot_peak[:, :, None, :], NEGATIVE)
    group_peak = jnp.max(spread, axis=1)
    slot_base = jnp.take(group_peak, owner_group, axis=1)
    weight = jnp.where(slot_used[None, :, None], jnp.exp(slot_peak - slot_base), 0.0)
    member_f = member.astype(jnp.float32)
    group_total = jnp.einsum(
        "sg,ksq->kgq", member_f, slot_total * weight, precision=lax.Precision.HIGHEST
    )
    group_acc = jnp.einsum(
        "sg,ksqd->kgqd", member_f, slot_acc * weight[..., None], precision=lax.Precision.HIGHEST
    )
    order_small = (2, 1, 3, 0, 4)
    peak_rows = jnp.transpose(
        group_peak.reshape(local_heads, GROUPS, num_steps, BEAMS, PER_KV), order_small
    )
    total_rows = jnp.transpose(
        group_total.reshape(local_heads, GROUPS, num_steps, BEAMS, PER_KV), order_small
    )
    acc_rows = jnp.transpose(
        group_acc.reshape(local_heads, GROUPS, num_steps, BEAMS, PER_KV, HEAD_DIM),
        (2, 1, 3, 0, 4, 5),
    )
    local_part = (peak_rows.reshape(-1), total_rows.reshape(-1), acc_rows.reshape(-1, HEAD_DIM))
    joined = merged(local_part, "pages", combine)
    complete = combine(joined, tail_part)
    attended = (complete[2] / complete[1][:, None]).astype(jnp.bfloat16)
    flat_heads = attended.reshape(row_count, local_heads * PER_KV * HEAD_DIM)
    head_terms = jnp.dot(flat_heads, w_out, preferred_element_type=jnp.float32)
    mixed_out = lax.psum(head_terms.astype(jnp.bfloat16), "kv").astype(jnp.float32) + widened
    return (mixed_out.astype(jnp.bfloat16).reshape(num_steps, num_seqs, -1), buffer)


def solution(mesh):
    placed = (
        P(),
        P(),
        P(),
        P(),
        P("kv", "pages"),
        P("pages"),
        P("pages", "kv"),
        P("kv", "pages"),
        P(None, None, None, "kv"),
        P(None, "pages", None, "kv"),
    )
    return jax.shard_map(
        per_device,
        mesh=mesh,
        in_specs=placed,
        out_specs=(P(None, None, "pages"), P(None, None, None, "kv")),
        check_vma=False,
    )
```

profile of v0, /device:TPU:1, one launch (start us, length us, event | category | flops | bytes accessed | tf_op | source)
XLA Modules:
  0.0 759.2 jit_solution(2022923756878189014)
XLA Ops:
  9.6 1.9 copy.93
  12.4 26.9 %psum.28 = bf16[128,112]{0,1:T(8,128)(2,1)S(1)} all-reduce(bf16[128,112]{0,1:T(8,128)(2,1)S(1)} %select_convert_fusion), channel_id=1, replica_groups=mesh['kv'=8,'pages'=64] {'kv'}, use_global_device_ids=true, to_apply=%region_3.4 | all-reduce | flops 14336 | bytes 57344 | tf_op jit(solution)/shard_map/psum | solution.py:83
  42.4 1.6 fusion.63
  45.4 119.0 %psum.30 = f32[128]{0:T(128)S(1)} all-reduce(f32[128]{0:T(128)S(1)} %fusion.34), channel_id=1, replica_groups=mesh['kv'=8,'pages'=64] {'pages'}, use_global_device_ids=true, to_apply=%region_6.7 | all-reduce | flops 128 | bytes 1024 | tf_op jit(solution)/shard_map/psum | solution.py:88
  164.5 5.0 fusion.54
  169.8 131.9 %all-reduce.3.cloned.1.call-done = f32[128,1152]{1,0:T(8,128)} async-done(((f32[128,1152]{1,0:T(8,128)}), f32[128,1152]{1,0:T(8,128)}) %all-reduce.3.cloned.1.call-update) | async-done | bytes 589840 | tf_op jit(solution)/shard_map/psum | solution.py:88
  309.3 1.4 copy.106
  311.9 1.6 gather_fusion.4
  315.4 67.5 %all-gather = f32[64,1,896]{2,1,0:T(1,128)S(1)} all-gather(f32[1,1,896]{2,1,0:T(1,128)S(1)} %reshape.757), channel_id=1, replica_groups=mesh['kv'=8,'pages'=64] {'pages'}, dimensions={0}, use_global_device_ids=true | all-gather | bytes 232960 | tf_op jit(solution)/shard_map/all_gather | solution.py:24
  383.6 72.0 %all-gather.1 = f32[64,1,896]{2,1,0:T(1,128)S(1)} all-gather(f32[1,1,896]{2,1,0:T(1,128)S(1)} %reshape.759), channel_id=1, replica_groups=mesh['kv'=8,'pages'=64] {'pages'}, dimensions={0}, use_global_device_ids=true | all-gather | bytes 232960 | tf_op jit(solution)/shard_map/all_gather | solution.py:24
  458.2 1.6 gather_fusion.5
  462.6 120.6 %all-gather.4.cloned.1.call-done = f32[64,896,128]{2,1,0:T(8,128)} async-done(((f32[1,896,128]{2,1,0:T(8,128)}), f32[64,896,128]{2,1,0:T(8,128)}) %all-gather.4.cloned.1.call-update) | async-done | bytes 29360144 | tf_op jit(solution)/shard_map/all_gather | solution.py:24
  584.3 142.8 %while.21 = (s32[]{:T(128)}, f32[896]{0:T(1024)S(1)}, f32[896]{0:T(1024)S(1)}, f32[896,128]{1,0:T(8,128)S(1)}, f32[64,896]{1,0:T(8,128)}, /*index=5*/f32[64,896]...) while((s32[]{:T(128)}, f32[896]{0:T(1024)S(1)}, f32[896]{0:T(1024)S(1)}, ...), condition=%wide.region_11.12_spmd, body=%wide.region_10.11_spmd.sunk | while | flops 349445 | bytes 1426575 | solution.py:29
  585.1 1.4 fusion.71
  587.4 1.4 fusion.71
  589.6 1.4 fusion.71
  591.9 1.4 fusion.71
  594.2 1.4 fusion.71
  596.4 1.4 fusion.71
  598.7 1.4 fusion.71
  601.0 1.4 fusion.71
  603.2 1.4 fusion.71
  605.5 1.4 fusion.71
  607.8 1.4 fusion.71
  610.0 1.4 fusion.71
  612.3 1.4 fusion.71
  619.1 1.4 fusion.71
  621.4 1.4 fusion.71
  630.4 1.4 fusion.71
  632.7 1.4 fusion.71
  639.5 1.4 fusion.71
  641.8 1.4 fusion.71
  650.8 1.4 fusion.71
  653.1 1.4 fusion.71
  662.1 1.4 fusion.71
  664.4 1.4 fusion.71
  673.5 1.4 fusion.71
  675.7 1.4 fusion.71
  682.5 1.4 fusion.71
  684.8 1.4 fusion.71
  693.9 1.4 fusion.71
  696.1 1.4 fusion.71
  705.2 1.4 fusion.71
  707.5 1.4 fusion.71
  716.5 1.4 fusion.71
  718.8 1.4 fusion.71
  725.6 1.4 fusion.71
  728.9 22.7 %psum.31 = bf16[128,112]{0,1:T(8,128)(2,1)S(1)} all-reduce(bf16[128,112]{0,1:T(8,128)(2,1)S(1)} %convolution_convert_fusion), channel_id=1, replica_groups=mesh['kv'=8,'pages'=64] {'kv'}, use_global_device_ids=true, to_apply=%region_14.16 | all-reduce | flops 14336 | bytes 57344 | tf_op jit(solution)/shard_map/psum | solution.py:199
  (247 shorter events, 120.3 us)
Async XLA Ops:
  7.2 32.2 %copy-start = (bf16[112,1152]{1,0:T(8,128)(2,1)S(1)}, bf16[112,1152]{1,0:T(8,128)(2,1)}, u32[]{:S(2)}) copy-start(bf16[112,1152]{1,0:T(8,128)(2,1)} %param.24) | copy-start | bytes 774148
  7.2 294.5 %all-reduce.3.cloned.1.call-start = ((), (), s32[]{:S(2)}) async-start(), calls=%async_computation | async-start | bytes 1179648 | tf_op jit(solution)/shard_map/psum | solution.py:88
  40.5 542.7 %all-gather.4.cloned.1.call-start = ((), (), s32[]{:S(2)}) async-start(), calls=%async_computation.1 | async-start | bytes 29818880 | tf_op jit(solution)/shard_map/all_gather | solution.py:24
Sparse Core Ops, SparseCore 0:
  40.6 261.0 all-reduce.2
  309.5 273.6 all-gather.3
where the time goes:
time: 768 us; the launch traced here: 759 us
  blocking collectives  308 us (40%)
  waiting for transfers between devices  253 us (33%)
  other arithmetic  104 us (14%)
  local copies, waits for them, and re-layouts  71.8 us (9%)
  between operations  14.5 us (2%)
    all_gather x2, blocking collectives, merged(): gathered = jax.tree.map(lambda a: lax.all_gather(a, axis), part)  139 us
    psum x1, waiting for transfers between devices, per_device(): summed, norm_sums = lax.psum((partial_value, squares), 'pages')  132 us
    all_gather x1, waiting for transfers between devices, merged(): gathered = jax.tree.map(lambda a: lax.all_gather(a, axis), part)  121 us
    psum x1, blocking collectives, per_device(): summed, norm_sums = lax.psum((partial_value, squares), 'pages')  119 us
    add x63, other arithmetic, combine(): earlier[2] * weight_one[:, None] + later[2] * weight_two[:, None]  89.9 us
    dynamic_slice x65, local copies, waits for them, and re-layouts, take(): lax.dynamic_index_in_dim(a, source, 0, False)  50.1 us
    psum x1, blocking collectives, per_device(): embedded = lax.psum(found.astype(jnp.bfloat16), 'kv')  26.9 us
    psum x1, blocking collectives, per_device(): lax.psum(head_terms.astype(jnp.bfloat16), 'kv').astype(jnp.float32)  22.7 us
  transfers between devices with their start and end apart: 2, of which 2 were waited for; matrix products, arithmetic and copies ran while one was open for 3% of the time, Pallas kernels for 0%

commit v1 on v0

--- a/solution.py
+++ b/solution.py
@@ -18,17 +18,6 @@
 THETA = 5000000.0
 EPSILON = 1e-05
 NEGATIVE = -1e30
-
-
-def merged(part, axis, combine):
-    gathered = jax.tree.map(lambda a: lax.all_gather(a, axis), part)
-
-    def take(source):
-        return jax.tree.map(lambda a: lax.dynamic_index_in_dim(a, source, 0, False), gathered)
-
-    return lax.fori_loop(
-        1, lax.axis_size(axis), lambda source, state: combine(state, take(source)), take(0)
-    )
 
 
 def rotate(values, positions):
@@ -67,11 +56,19 @@
     )
 
 
+def reduce_rows(packed, axis):
+    sources = lax.axis_size(axis)
+    split = packed.reshape(sources, packed.shape[0] // sources, *packed.shape[1:])
+    return jnp.sum(lax.all_to_all(split, axis, 0, 0, tiled=False), axis=0)
+
+
 def per_device(
     tokens, prompt_len, page_table, parents, embedding, norm_gain, w_qkv, w_out, history, kv_pool
 ):
     num_steps, num_seqs = tokens.shape
     row_count = num_steps * num_seqs
+    page_devices = lax.axis_size("pages")
+    page_index = lax.axis_index("pages")
     local_heads = KV_HEADS // lax.axis_size("kv")
     kv_width = local_heads * HEAD_DIM
     inv_root = 1.0 / jnp.sqrt(jnp.float32(HEAD_DIM))
@@ -79,16 +76,25 @@
     local_ids = tokens.reshape(-1) - lax.axis_index("kv") * vocab_local
     inside = (local_ids >= 0) & (local_ids < vocab_local)
     picked = jnp.take(embedding, jnp.clip(local_ids, 0, vocab_local - 1), axis=0)
-    found = jnp.where(inside[:, None], picked.astype(jnp.float32), 0.0)
-    embedded = lax.psum(found.astype(jnp.bfloat16), "kv")
+    found = jnp.where(inside[:, None], picked, jnp.zeros_like(picked))
+    embedded = lax.psum(found, "kv")
     widened = embedded.astype(jnp.float32)
     squares = jnp.sum(widened * widened, axis=1)
     normed = (widened * norm_gain.astype(jnp.float32)).astype(jnp.bfloat16)
     partial_value = jnp.dot(normed, w_qkv, preferred_element_type=jnp.float32)
-    summed, norm_sums = lax.psum((partial_value, squares), "pages")
-    projected = finish_rows(
-        summed, norm_sums, jnp.arange(row_count, dtype=jnp.int32), prompt_len, num_seqs, local_heads
-    )
+    qkv_cols = partial_value.shape[1]
+    packed = jnp.concatenate(
+        [partial_value, squares[:, None], jnp.zeros((row_count, 127), jnp.float32)], axis=1
+    )
+    reduced = reduce_rows(packed, "pages")
+    rows_per = row_count // page_devices
+    my_rows = page_index * rows_per + jnp.arange(rows_per, dtype=jnp.int32)
+    mine = finish_rows(
+        reduced[:, :qkv_cols], reduced[:, qkv_cols], my_rows, prompt_len, num_seqs, local_heads
+    )
+    projected = lax.all_gather(
+        mine.reshape(rows_per, qkv_cols), "pages", axis=0, tiled=True
+    ).reshape(row_count, local_heads, PER_KV + 2, HEAD_DIM)
     queries = projected[:, :, :PER_KV]
     fresh_kv = jnp.stack([projected[:, :, PER_KV], projected[:, :, PER_KV + 1]]).reshape(
         2, num_steps, num_seqs, kv_width
@@ -125,7 +131,7 @@
     )
     tail_part = (tail_peak.reshape(-1), tail_total.reshape(-1), tail_acc.reshape(-1, HEAD_DIM))
     slot_rows = kv_pool.shape[1]
-    slot_ids = lax.axis_index("pages") * slot_rows + jnp.arange(slot_rows, dtype=jnp.int32)
+    slot_ids = page_index * slot_rows + jnp.arange(slot_rows, dtype=jnp.int32)
     matches = page_table[:, :, None] == slot_ids[None, None, :]
     slot_used = jnp.any(matches, axis=(0, 1))
     owner_group = jnp.sum(
@@ -191,12 +197,28 @@
         (2, 1, 3, 0, 4, 5),
     )
     local_part = (peak_rows.reshape(-1), total_rows.reshape(-1), acc_rows.reshape(-1, HEAD_DIM))
-    joined = merged(local_part, "pages", combine)
-    complete = combine(joined, tail_part)
-    attended = (complete[2] / complete[1][:, None]).astype(jnp.bfloat16)
+    with_tail = combine(local_part, tail_part)
+    first = page_index == 0
+    part = jax.tree.map(lambda a, b: jnp.where(first, a, b), with_tail, local_part)
+    attn_rows = part[0].shape[0]
+    share = attn_rows // page_devices
+    stats = jnp.zeros((page_devices, 2, HEAD_DIM), jnp.float32)
+    stats = stats.at[:, 0, :share].set(part[0].reshape(page_devices, share))
+    stats = stats.at[:, 1, :share].set(part[1].reshape(page_devices, share))
+    sent = jnp.concatenate([part[2].reshape(page_devices, share, HEAD_DIM), stats], axis=1)
+    received = lax.all_to_all(sent, "pages", 0, 0, tiled=False)
+    src_acc = received[:, :share]
+    src_peak = received[:, share, :share]
+    src_total = received[:, share + 1, :share]
+    top = jnp.max(src_peak, axis=0)
+    scale = jnp.exp(src_peak - top[None, :])
+    total = jnp.sum(src_total * scale, axis=0)
+    acc = jnp.sum(src_acc * scale[:, :, None], axis=0)
+    attended_mine = (acc / total[:, None]).astype(jnp.bfloat16)
+    attended = lax.all_gather(attended_mine, "pages", axis=0, tiled=True)
     flat_heads = attended.reshape(row_count, local_heads * PER_KV * HEAD_DIM)
     head_terms = jnp.dot(flat_heads, w_out, preferred_element_type=jnp.float32)
-    mixed_out = lax.psum(head_terms.astype(jnp.bfloat16), "kv").astype(jnp.float32) + widened
+    mixed_out = lax.psum(head_terms, "kv") + widened
     return (mixed_out.astype(jnp.bfloat16).reshape(num_steps, num_seqs, -1), buffer)
 
 

time: 768 us -> 331 us (0.43)
  waiting for transfers between devices: 253 us -> 45.9 us
  other arithmetic: 104 us -> 4.29 us
  blocking collectives: 308 us -> 229 us
  local copies, waits for them, and re-layouts: 71.8 us -> 21.8 us
  starting transfers between devices: 0.08 us -> 25 us
  between operations: 14.5 us -> 1.18 us
    psum x1 -> x0, waiting for transfers between devices: 132 us -> none  [per_device(): summed, norm_sums = lax.psum((partial_value, squares), 'pages')]
    all_gather x1 -> x0, waiting for transfers between devices: 121 us -> none  [merged(): gathered = jax.tree.map(lambda a: lax.all_gather(a, axis), part)]
    add x128 -> x1, other arithmetic: 90.7 us -> 0.01 us  [per_device(): slot_ids = page_index * slot_rows + jnp.arange(slot_rows, dtype=jnp.int32)]
    psum x3 -> x2, blocking collectives: 169 us -> 93.7 us  [the longest x1 66.7 us: per_device(): mixed_out = lax.psum(head_terms, 'kv') + widened]
    dynamic_slice x65 -> x0, local copies, waits for them, and re-layouts: 50.1 us -> none  [take(): lax.dynamic_index_in_dim(a, source, 0, False)]
    all_to_all x0 -> x2, waiting for transfers between devices: none -> 45.9 us  [the longest x1 26.3 us: reduce_rows(): return jnp.sum(lax.all_to_all(split, axis, 0, 0, tiled=False), axis=0)]
    all_to_all x0 -> x2, starting transfers between devices: none -> 25 us  [the longest x1 15.3 us: reduce_rows(): return jnp.sum(lax.all_to_all(split, axis, 0, 0, tiled=False), axis=0)]
  transfers between devices with their start and end apart: 2 -> 2, of which waited for: 2 -> 2; matrix products, arithmetic and copies ran while one was open for 3% -> 2% of each run, Pallas kernels for 0% -> 0%
where the time goes in v1:
time: 331 us; the launch traced here: 330 us
  blocking collectives  229 us (69%)
  waiting for transfers between devices  45.9 us (14%)
  starting transfers between devices  25 us (8%)
  local copies, waits for them, and re-layouts  21.8 us (7%)
  other arithmetic  4.29 us (1%)
    all_gather x1, blocking collectives, per_device(): lax.all_gather(mine.reshape(rows_per, qkv_cols), 'pages', axis=0, tiled=T...  69 us
    psum x1, blocking collectives, per_device(): mixed_out = lax.psum(head_terms, 'kv') + widened  66.7 us
    all_gather x1, blocking collectives, per_device(): attended = lax.all_gather(attended_mine, 'pages', axis=0, tiled=True)  66.2 us
    psum x1, blocking collectives, per_device(): embedded = lax.psum(found, 'kv')  26.9 us
    all_to_all x1, waiting for transfers between devices, reduce_rows(): return jnp.sum(lax.all_to_all(split, axis, 0, 0, tiled=False), axis=0)  26.3 us
    all_to_all x1, waiting for transfers between devices, per_device(): received = lax.all_to_all(sent, 'pages', 0, 0, tiled=False)  19.6 us
    all_to_all x1, starting transfers between devices, reduce_rows(): return jnp.sum(lax.all_to_all(split, axis, 0, 0, tiled=False), axis=0)  15.3 us
    all_to_all x1, starting transfers between devices, per_device(): received = lax.all_to_all(sent, 'pages', 0, 0, tiled=False)  9.7 us
  transfers between devices with their start and end apart: 2, of which 2 were waited for; matrix products, arithmetic and copies ran while one was open for 2% of the time, Pallas kernels for 0%

profile of v1, /device:TPU:1, one launch (start us, length us, event | category | flops | bytes accessed | tf_op | source)
XLA Modules:
  0.0 329.8 jit_solution(9333004491464431049)
XLA Ops:
  0.7 0.7 copy-done.6
  1.6 0.6 copy-done.8
  2.2 1.9 copy.207
  4.2 0.7 gather_fusion.1
  5.0 26.9 %psum.14 = bf16[128,112]{0,1:T(8,128)(2,1)S(1)} all-reduce(bf16[128,112]{0,1:T(8,128)(2,1)S(1)} %select_select_fusion), channel_id=1, replica_groups=mesh['kv'=8,'pages'=64] {'kv'}, use_global_device_ids=true, to_apply=%region_3.4 | all-reduce | flops 14336 | bytes 57344 | tf_op jit(solution)/shard_map/psum | solution.py:80
  32.0 0.3 concatenate.41
  32.3 0.3 fusion.42
  32.6 0.3 concatenate.34
  33.0 2.2 concatenate.36
  35.2 15.3 %all-to-all-start = ((f32[64,2,1280]{2,1,0:T(2,128)}), f32[64,2,1280]{2,1,0:T(2,128)S(1)}, u32[]{:S(2)}, u32[]{:S(2)}) async-start(f32[64,2,1280]{2,1,0:T(2,128)} %concatenate.36), calls=%async_computation | async-start | bytes 1310720 | tf_op jit(solution)/shard_map/all_to_all | solution.py:62
  50.5 0.7 copy-done.5
  51.2 0.2 compare_reduce_fusion
  51.4 0.2 fusion.37
  51.7 0.6 gather_fusion
  52.4 0.6 gather_fusion.2
  53.0 0.4 copy.218
  53.5 0.3 concatenate.39
  53.8 0.3 copy-done.7
  54.2 1.6 gather_fusion.5
  56.2 26.3 %all-to-all-done = f32[64,2,1280]{2,1,0:T(2,128)S(1)} async-done(((f32[64,2,1280]{2,1,0:T(2,128)}), f32[64,2,1280]{2,1,0:T(2,128)S(1)}, u32[]{:S(2)}, u32[]{:S(2)}) %all-to-all-start) | async-done | bytes 655392 | tf_op jit(solution)/shard_map/all_to_all | solution.py:62
  82.5 0.2 reduce_sum.78
  83.1 69.0 %all-gather = bf16[64,2,1152]{2,1,0:T(2,128)(2,1)S(1)} all-gather(bf16[1,2,1152]{2,1,0:T(2,128)(2,1)S(1)} %reshape.977), channel_id=1, replica_groups=mesh['kv'=8,'pages'=64] {'pages'}, dimensions={0}, use_global_device_ids=true | all-gather | bytes 299520 | tf_op jit(solution)/shard_map/all_gather | solution.py:95
  152.1 0.2 reshape.889
  152.5 0.6 gather_fusion.3
  153.3 0.9 copy-done.4
  154.2 0.4 fusion.65
  154.6 0.6 gather_fusion.4
  155.5 1.4 scatter.14
  156.9 0.5 copy.221
  157.4 1.6 gather_fusion.6
  159.3 0.5 fusion.66
  159.7 0.4 fusion.7
  160.1 0.4 fusion.14
  160.7 0.4 fusion.16
  161.1 0.4 convolution_multiply_fusion.1
  161.5 0.4 fusion.12
  163.1 0.3 add_select_fusion
  163.4 0.9 pad_maximum_fusion.1
  164.3 9.7 %all-to-all-start.1 = ((f32[64,16,128]{2,1,0:T(8,128)}), f32[64,16,128]{2,1,0:T(8,128)S(1)}, u32[]{:S(2)}, u32[]{:S(2)}) async-start(f32[64,16,128]{2,1,0:T(8,128)} %pad_maximum_fusion.1), calls=%async_computation.1 | async-start | bytes 1048576 | tf_op jit(solution)/shard_map/all_to_all | solution.py:209
  174.0 0.9 copy.237
  174.9 19.6 %all-to-all-done.1 = f32[64,16,128]{2,1,0:T(8,128)S(1)} async-done(((f32[64,16,128]{2,1,0:T(8,128)}), f32[64,16,128]{2,1,0:T(8,128)S(1)}, u32[]{:S(2)}, u32[]{:S(2)}) %all-to-all-start.1) | async-done | bytes 524320 | tf_op jit(solution)/shard_map/all_to_all | solution.py:209
  194.6 0.2 fusion.5
  194.9 66.2 %all-gather.1 = bf16[64,14,128]{2,1,0:T(8,128)(2,1)S(1)} all-gather(bf16[1,14,128]{2,1,0:T(8,128)(2,1)S(1)} %fusion.46), channel_id=1, replica_groups=mesh['kv'=8,'pages'=64] {'pages'}, dimensions={0}, use_global_device_ids=true | all-gather | bytes 232960 | tf_op jit(solution)/shard_map/all_gather | solution.py:218
  261.1 0.3 reshape.910
  261.4 0.7 copy-done.3
  262.1 0.2 fusion.67
  262.3 66.7 %psum.15 = f32[128,112]{0,1:T(8,128)S(1)} all-reduce(f32[128,112]{0,1:T(8,128)S(1)} %fusion.67), channel_id=1, replica_groups=mesh['kv'=8,'pages'=64] {'kv'}, use_global_device_ids=true, to_apply=%region_14.16 | all-reduce | flops 14336 | bytes 114688 | tf_op jit(solution)/shard_map/psum | solution.py:221
  329.0 0.7 copy.236
  (90 shorter events, 4.0 us)
Async XLA Ops:
  0.6 31.7 %copy-start = (bf16[112,1152]{1,0:T(8,128)(2,1)S(1)}, bf16[112,1152]{1,0:T(8,128)(2,1)}, u32[]{:S(2)}) copy-start(bf16[112,1152]{1,0:T(8,128)(2,1)} %param.26) | copy-start | bytes 774148
  0.7 0.7 copy-start.6
  1.5 0.7 copy-start.8
  35.2 16.5 %copy-start.1 = (s32[8]{0:T(128)S(1)}, s32[8]{0:T(128)}, u32[]{:S(2)}) copy-start(s32[8]{0:T(128)} %param.21) | copy-start | bytes 100
  35.2 47.3 %all-to-all-start = ((f32[64,2,1280]{2,1,0:T(2,128)}), f32[64,2,1280]{2,1,0:T(2,128)S(1)}, u32[]{:S(2)}, u32[]{:S(2)}) async-start(f32[64,2,1280]{2,1,0:T(2,128)} %concatenate.36), calls=%async_computation | async-start | bytes 1310720 | tf_op jit(solution)/shard_map/all_to_all | solution.py:62
  50.5 0.7 copy-start.5
  51.7 1.3 copy-start.2
  53.5 0.7 copy-start.7
  153.1 1.0 copy-start.4
  164.3 30.3 %all-to-all-start.1 = ((f32[64,16,128]{2,1,0:T(8,128)}), f32[64,16,128]{2,1,0:T(8,128)S(1)}, u32[]{:S(2)}, u32[]{:S(2)}) async-start(f32[64,16,128]{2,1,0:T(8,128)} %pad_maximum_fusion.1), calls=%async_computation.1 | async-start | bytes 1048576 | tf_op jit(solution)/shard_map/all_to_all | solution.py:209
  261.1 0.9 copy-start.3

commit v2 on v1

--- a/solution.py
+++ b/solution.py
@@ -54,6 +54,12 @@
         earlier[1] * weight_one + later[1] * weight_two,
         earlier[2] * weight_one[:, None] + later[2] * weight_two[:, None],
     )
+
+
+def gather_all(part, axis):
+    count = lax.axis_size(axis)
+    spread = jnp.broadcast_to(part[None], (count, *part.shape))
+    return lax.all_to_all(spread, axis, 0, 0, tiled=False)
 
 
 def reduce_rows(packed, axis):
@@ -77,8 +83,7 @@
     inside = (local_ids >= 0) & (local_ids < vocab_local)
     picked = jnp.take(embedding, jnp.clip(local_ids, 0, vocab_local - 1), axis=0)
     found = jnp.where(inside[:, None], picked, jnp.zeros_like(picked))
-    embedded = lax.psum(found, "kv")
-    widened = embedded.astype(jnp.float32)
+    widened = jnp.sum(gather_all(found, "kv").astype(jnp.float32), axis=0)
     squares = jnp.sum(widened * widened, axis=1)
     normed = (widened * norm_gain.astype(jnp.float32)).astype(jnp.bfloat16)
     partial_value = jnp.dot(normed, w_qkv, preferred_element_type=jnp.float32)
@@ -92,9 +97,9 @@
     mine = finish_rows(
         reduced[:, :qkv_cols], reduced[:, qkv_cols], my_rows, prompt_len, num_seqs, local_heads
     )
-    projected = lax.all_gather(
-        mine.reshape(rows_per, qkv_cols), "pages", axis=0, tiled=True
-    ).reshape(row_count, local_heads, PER_KV + 2, HEAD_DIM)
+    projected = gather_all(mine.reshape(rows_per, qkv_cols), "pages").reshape(
+        row_count, local_heads, PER_KV + 2, HEAD_DIM
+    )
     queries = projected[:, :, :PER_KV]
     fresh_kv = jnp.stack([projected[:, :, PER_KV], projected[:, :, PER_KV + 1]]).reshape(
         2, num_steps, num_seqs, kv_width
@@ -215,10 +220,10 @@
     total = jnp.sum(src_total * scale, axis=0)
     acc = jnp.sum(src_acc * scale[:, :, None], axis=0)
     attended_mine = (acc / total[:, None]).astype(jnp.bfloat16)
-    attended = lax.all_gather(attended_mine, "pages", axis=0, tiled=True)
+    attended = gather_all(attended_mine, "pages")
     flat_heads = attended.reshape(row_count, local_heads * PER_KV * HEAD_DIM)
     head_terms = jnp.dot(flat_heads, w_out, preferred_element_type=jnp.float32)
-    mixed_out = lax.psum(head_terms, "kv") + widened
+    mixed_out = jnp.sum(gather_all(head_terms, "kv"), axis=0) + widened
     return (mixed_out.astype(jnp.bfloat16).reshape(num_steps, num_seqs, -1), buffer)
 
 

time: 331 us -> 199 us (0.60)
  blocking collectives: 229 us -> 64.4 us
  waiting for transfers between devices: 45.9 us -> 62.5 us
  starting transfers between devices: 25 us -> 40.6 us
    all_gather x2 -> x0, blocking collectives: 135 us -> none  [the longest x1 69 us: per_device(): lax.all_gather(mine.reshape(rows_per, qkv_cols), 'pages', axis=0, tiled=T...]
    psum x2 -> x0, blocking collectives: 93.7 us -> none  [the longest x1 66.7 us: per_device(): mixed_out = lax.psum(head_terms, 'kv') + widened]
    all_to_all x0 -> x2, blocking collectives: none -> 64.4 us  [the longest x1 36.8 us: per_device(): received = lax.all_to_all(sent, 'pages', 0, 0, tiled=False)]
    all_to_all x1 -> x3, starting transfers between devices: 9.7 us -> 26.4 us  [gather_all(): return lax.all_to_all(spread, axis, 0, 0, tiled=False)]
    all_to_all x1 -> x3, waiting for transfers between devices: 19.6 us -> 30.2 us  [gather_all(): return lax.all_to_all(spread, axis, 0, 0, tiled=False)]
    all_to_all x1, waiting for transfers between devices: 26.3 us -> 32.3 us  [reduce_rows(): return jnp.sum(lax.all_to_all(split, axis, 0, 0, tiled=False), axis=0)]
  transfers between devices with their start and end apart: 2 -> 4, of which waited for: 2 -> 4; matrix products, arithmetic and copies ran while one was open for 2% -> 3% of each run, Pallas kernels for 0% -> 0%
where the time goes in v2:
time: 199 us; the launch traced here: 198 us
  blocking collectives  64.4 us (32%)
  waiting for transfers between devices  62.5 us (31%)
  starting transfers between devices  40.6 us (20%)
  local copies, waits for them, and re-layouts  23.4 us (12%)
  other arithmetic  3.65 us (2%)
  matrix products  2.64 us (1%)
    all_to_all x1, blocking collectives, per_device(): received = lax.all_to_all(sent, 'pages', 0, 0, tiled=False)  36.8 us
    all_to_all x1, waiting for transfers between devices, reduce_rows(): return jnp.sum(lax.all_to_all(split, axis, 0, 0, tiled=False), axis=0)  32.3 us
    all_to_all x3, waiting for transfers between devices, gather_all(): return lax.all_to_all(spread, axis, 0, 0, tiled=False)  30.2 us
    all_to_all x1, blocking collectives, gather_all(): return lax.all_to_all(spread, axis, 0, 0, tiled=False)  27.6 us
    all_to_all x3, starting transfers between devices, gather_all(): return lax.all_to_all(spread, axis, 0, 0, tiled=False)  26.4 us
    all_to_all x1, starting transfers between devices, reduce_rows(): return jnp.sum(lax.all_to_all(split, axis, 0, 0, tiled=False), axis=0)  14.2 us
    unnamed x24, local copies, waits for them, and re-layouts  6.27 us
  transfers between devices with their start and end apart: 4, of which 4 were waited for; matrix products, arithmetic and copies ran while one was open for 3% of the time, Pallas kernels for 0%

profile of v2, /device:TPU:1, one launch (start us, length us, event | category | flops | bytes accessed | tf_op | source)
XLA Modules:
  0.0 198.4 jit_solution(13828545118437900696)
XLA Ops:
  0.7 0.7 copy-done.6
  1.7 1.9 copy.260
  3.6 0.7 gather_fusion.1
  4.5 0.7 broadcast_in_dim.217
  5.3 10.3 %all-to-all-start = ((bf16[8,128,112]{1,2,0:T(8,128)(2,1)}), bf16[8,128,112]{1,2,0:T(8,128)(2,1)S(1)}, u32[]{:S(2)}, u32[]{:S(2)}) async-start(bf16[8,128,112]{1,2,0:T(8,128)(2,1)} %broadcast_in_dim.217), calls=%async_computation | async-start | bytes 458752 | tf_op jit(solution)/shard_map/all_to_all | solution.py:62
  15.6 6.2 %all-to-all-done = bf16[8,128,112]{1,2,0:T(8,128)(2,1)S(1)} async-done(((bf16[8,128,112]{1,2,0:T(8,128)(2,1)}), bf16[8,128,112]{1,2,0:T(8,128)(2,1)S(1)}, u32[]{:S(2)}, u32[]{:S(2)}) %all-to-all-start) | async-done | bytes 229408 | tf_op jit(solution)/shard_map/all_to_all | solution.py:62
  21.8 0.3 concatenate.41
  22.1 0.3 fusion.39
  22.4 0.3 concatenate.34
  22.8 2.2 %concatenate.36 = f32[64,2,1280]{2,1,0:T(2,128)} concatenate(f32[64,2,1152]{2,1,0:T(2,128)S(1)} %concatenate.34, f32[64,2,1]{2,1,0:T(2,128)S(1)} %concatenate.41, f32[64,2,127]{2,1,0:T(2,128)S(1)} %broadcast_in_dim.218), dimensions={2} | concatenate | bytes 1310720 | tf_op jit(solution)/shard_map/concatenate | solution.py:91
  25.0 14.2 %all-to-all-start.1 = ((f32[64,2,1280]{2,1,0:T(2,128)}), f32[64,2,1280]{2,1,0:T(2,128)S(1)}, u32[]{:S(2)}, u32[]{:S(2)}) async-start(f32[64,2,1280]{2,1,0:T(2,128)} %concatenate.36), calls=%async_computation.1 | async-start | bytes 1310720 | tf_op jit(solution)/shard_map/all_to_all | solution.py:68
  39.2 0.6 gather_fusion.2
  40.4 0.7 copy-done.7
  41.1 32.3 %all-to-all-done.1 = f32[64,2,1280]{2,1,0:T(2,128)S(1)} async-done(((f32[64,2,1280]{2,1,0:T(2,128)}), f32[64,2,1280]{2,1,0:T(2,128)S(1)}, u32[]{:S(2)}, u32[]{:S(2)}) %all-to-all-start.1) | async-done | bytes 655392 | tf_op jit(solution)/shard_map/all_to_all | solution.py:68
  73.5 0.2 reduce_sum.97
  74.1 0.9 broadcast_in_dim.219
  75.0 9.5 %all-to-all-start.2 = ((bf16[64,2,1152]{2,1,0:T(2,128)(2,1)}), bf16[64,2,1152]{2,1,0:T(2,128)(2,1)S(1)}, u32[]{:S(2)}, u32[]{:S(2)}) async-start(bf16[64,2,1152]{2,1,0:T(2,128)(2,1)} %broadcast_in_dim.219), calls=%async_computation.2 | async-start | bytes 589824 | tf_op jit(solution)/shard_map/all_to_all | solution.py:62
  84.6 0.6 gather_fusion
  85.3 0.4 copy.271
  85.7 0.3 concatenate.39
  86.1 1.6 gather_fusion.5
  87.9 16.2 %all-to-all-done.2 = bf16[64,2,1152]{2,1,0:T(2,128)(2,1)S(1)} async-done(((bf16[64,2,1152]{2,1,0:T(2,128)(2,1)}), bf16[64,2,1152]{2,1,0:T(2,128)(2,1)S(1)}, u32[]{:S(2)}, u32[]{:S(2)}) %all-to-all-start.2) | async-done | bytes 294944 | tf_op jit(solution)/shard_map/all_to_all | solution.py:62
  104.2 0.2 reshape.934
  104.6 0.6 gather_fusion.3
  105.3 0.9 copy-done.4
  106.2 0.4 fusion.60
  106.7 0.6 gather_fusion.4
  107.6 1.4 scatter.14
  109.0 0.5 copy.274
  109.5 1.6 gather_fusion.6
  111.3 0.5 fusion.61
  111.8 0.4 fusion.7
  112.1 0.4 fusion.14
  112.7 0.4 fusion.16
  113.1 0.3 convolution_multiply_fusion.1
  113.6 0.4 fusion.12
  115.1 0.3 add_select_fusion
  115.5 36.8 %all_to_all.30 = f32[64,16,128]{2,1,0:T(8,128)S(1)} all-to-all(f32[64,16,128]{2,1,0:T(8,128)S(1)} %pad_maximum_fusion.1), channel_id=1, replica_groups=mesh['kv'=8,'pages'=64] {'pages'}, dimensions={0} | all-to-all | bytes 1048576 | tf_op jit(solution)/shard_map/all_to_all | solution.py:214
  152.4 0.2 fusion.5
  152.8 27.6 %all_to_all.31 = bf16[64,14,128]{2,1,0:T(8,128)(2,1)S(1)} all-to-all(bf16[64,14,128]{2,1,0:T(8,128)(2,1)S(1)} %broadcast_in_dim.233), channel_id=1, replica_groups=mesh['kv'=8,'pages'=64] {'pages'}, dimensions={0} | all-to-all | bytes 458752 | tf_op jit(solution)/shard_map/all_to_all | solution.py:62
  180.4 0.3 reshape.955
  180.6 0.7 copy-done.3
  181.3 0.2 fusion.62
  181.5 0.8 broadcast_in_dim.234
  182.3 6.6 %all-to-all-start.5 = ((f32[8,128,112]{1,2,0:T(8,128)}), f32[8,128,112]{1,2,0:T(8,128)S(1)}, u32[]{:S(2)}, u32[]{:S(2)}) async-start(f32[8,128,112]{1,2,0:T(8,128)} %broadcast_in_dim.234), calls=%async_computation.5 | async-start | bytes 917504 | tf_op jit(solution)/shard_map/all_to_all | solution.py:62
  188.9 0.9 copy.290
  189.8 7.8 %all-to-all-done.5 = f32[8,128,112]{1,2,0:T(8,128)S(1)} async-done(((f32[8,128,112]{1,2,0:T(8,128)}), f32[8,128,112]{1,2,0:T(8,128)S(1)}, u32[]{:S(2)}, u32[]{:S(2)}) %all-to-all-start.5) | async-done | bytes 458784 | tf_op jit(solution)/shard_map/all_to_all | solution.py:62
  197.6 0.7 copy.289
  (98 shorter events, 4.6 us)
Async XLA Ops:
  0.6 21.4 %copy-start = (bf16[112,1152]{1,0:T(8,128)(2,1)S(1)}, bf16[112,1152]{1,0:T(8,128)(2,1)}, u32[]{:S(2)}) copy-start(bf16[112,1152]{1,0:T(8,128)(2,1)} %param.26) | copy-start | bytes 774148
  0.7 0.7 copy-start.6
  5.3 10.3 %copy-start.8 = (bf16[112]{0:T(256)(128)(2,1)S(1)}, bf16[112]{0:T(256)(128)(2,1)}, u32[]{:S(2)}) copy-start(bf16[112]{0:T(256)(128)(2,1)} %param.25) | copy-start | bytes 676
  5.3 16.5 %all-to-all-start = ((bf16[8,128,112]{1,2,0:T(8,128)(2,1)}), bf16[8,128,112]{1,2,0:T(8,128)(2,1)S(1)}, u32[]{:S(2)}, u32[]{:S(2)}) async-start(bf16[8,128,112]{1,2,0:T(8,128)(2,1)} %broadcast_in_dim.217), calls=%async_computation | async-start | bytes 458752 | tf_op jit(solution)/shard_map/all_to_all | solution.py:62
  25.0 14.3 %copy-start.1 = (s32[8]{0:T(128)S(1)}, s32[8]{0:T(128)}, u32[]{:S(2)}) copy-start(s32[8]{0:T(128)} %param.21) | copy-start | bytes 100
  25.0 48.5 %all-to-all-start.1 = ((f32[64,2,1280]{2,1,0:T(2,128)}), f32[64,2,1280]{2,1,0:T(2,128)S(1)}, u32[]{:S(2)}, u32[]{:S(2)}) async-start(f32[64,2,1280]{2,1,0:T(2,128)} %concatenate.36), calls=%async_computation.1 | async-start | bytes 1310720 | tf_op jit(solution)/shard_map/all_to_all | solution.py:68
  39.2 0.7 copy-start.5
  40.3 0.7 copy-start.7
  75.0 10.3 %copy-start.2 = (bf16[2,64,13,128]{3,1,2,0:T(8,128)(2,1)S(1)}, bf16[2,64,13,128]{3,1,2,0:T(8,128)(2,1)}, u32[]{:S(2)}) copy-start(bf16[2,64,13,128]{3,1,2,0:T(8,128)(2,1)} %param.28) | copy-start | bytes 1277956
  75.0 29.2 %all-to-all-start.2 = ((bf16[64,2,1152]{2,1,0:T(2,128)(2,1)}), bf16[64,2,1152]{2,1,0:T(2,128)(2,1)S(1)}, u32[]{:S(2)}, u32[]{:S(2)}) async-start(bf16[64,2,1152]{2,1,0:T(2,128)(2,1)} %broadcast_in_dim.219), calls=%async_computation.2 | async-start | bytes 589824 | tf_op jit(solution)/shard_map/all_to_all | solution.py:62
  105.2 1.0 copy-start.4
  180.4 0.9 copy-start.3
  182.3 15.3 %all-to-all-start.5 = ((f32[8,128,112]{1,2,0:T(8,128)}), f32[8,128,112]{1,2,0:T(8,128)S(1)}, u32[]{:S(2)}, u32[]{:S(2)}) async-start(f32[8,128,112]{1,2,0:T(8,128)} %broadcast_in_dim.234), calls=%async_computation.5 | async-start | bytes 917504 | tf_op jit(solution)/shard_map/all_to_all | solution.py:62

commit v3 on v2

--- a/solution.py
+++ b/solution.py
@@ -1,7 +1,7 @@
 import jax
 import jax.numpy as jnp
 from jax import lax
-from jax.sharding import PartitionSpec as P
+from jax.sharding import Mesh, PartitionSpec as P
 
 D = 7168
 KV_HEADS = 8
@@ -62,10 +62,35 @@
     return lax.all_to_all(spread, axis, 0, 0, tiled=False)
 
 
-def reduce_rows(packed, axis):
-    sources = lax.axis_size(axis)
-    split = packed.reshape(sources, packed.shape[0] // sources, *packed.shape[1:])
-    return jnp.sum(lax.all_to_all(split, axis, 0, 0, tiled=False), axis=0)
+def gather_rows(part):
+    inner = gather_all(part, "pz")
+    inner = inner.reshape(-1, *part.shape[1:])
+    outer = gather_all(inner, "px")
+    return outer.reshape(-1, *part.shape[1:])
+
+
+def reduce_rows(packed):
+    for axis in ("px", "pz"):
+        sources = lax.axis_size(axis)
+        split = packed.reshape(sources, packed.shape[0] // sources, *packed.shape[1:])
+        packed = jnp.sum(lax.all_to_all(split, axis, 0, 0, tiled=False), axis=0)
+    return packed
+
+
+def merge_blocks(received, share):
+    peak = received[:, ..., share, :share]
+    top = jnp.max(peak, axis=0)
+    scale = jnp.exp(peak - top[None])
+    total = jnp.sum(received[:, ..., share + 1, :share] * scale, axis=0)
+    acc = jnp.sum(received[:, ..., :share, :] * scale[..., None], axis=0)
+    return top, total, acc
+
+
+def pack_blocks(top, total, acc, share):
+    stats = jnp.zeros((*acc.shape[:-2], 2, HEAD_DIM), jnp.float32)
+    stats = stats.at[..., 0, :share].set(top)
+    stats = stats.at[..., 1, :share].set(total)
+    return jnp.concatenate([acc, stats], axis=-2)
 
 
 def per_device(
@@ -73,8 +98,10 @@
 ):
     num_steps, num_seqs = tokens.shape
     row_count = num_steps * num_seqs
-    page_devices = lax.axis_size("pages")
-    page_index = lax.axis_index("pages")
+    outer_count = lax.axis_size("px")
+    inner_count = lax.axis_size("pz")
+    page_devices = outer_count * inner_count
+    page_index = lax.axis_index("px") * inner_count + lax.axis_index("pz")
     local_heads = KV_HEADS // lax.axis_size("kv")
     kv_width = local_heads * HEAD_DIM
     inv_root = 1.0 / jnp.sqrt(jnp.float32(HEAD_DIM))
@@ -91,13 +118,13 @@
     packed = jnp.concatenate(
         [partial_value, squares[:, None], jnp.zeros((row_count, 127), jnp.float32)], axis=1
     )
-    reduced = reduce_rows(packed, "pages")
+    reduced = reduce_rows(packed)
     rows_per = row_count // page_devices
     my_rows = page_index * rows_per + jnp.arange(rows_per, dtype=jnp.int32)
     mine = finish_rows(
         reduced[:, :qkv_cols], reduced[:, qkv_cols], my_rows, prompt_len, num_seqs, local_heads
     )
-    projected = gather_all(mine.reshape(rows_per, qkv_cols), "pages").reshape(
+    projected = gather_rows(mine.reshape(rows_per, qkv_cols)).reshape(
         row_count, local_heads, PER_KV + 2, HEAD_DIM
     )
     queries = projected[:, :, :PER_KV]
@@ -207,20 +234,17 @@
     part = jax.tree.map(lambda a, b: jnp.where(first, a, b), with_tail, local_part)
     attn_rows = part[0].shape[0]
     share = attn_rows // page_devices
-    stats = jnp.zeros((page_devices, 2, HEAD_DIM), jnp.float32)
-    stats = stats.at[:, 0, :share].set(part[0].reshape(page_devices, share))
-    stats = stats.at[:, 1, :share].set(part[1].reshape(page_devices, share))
-    sent = jnp.concatenate([part[2].reshape(page_devices, share, HEAD_DIM), stats], axis=1)
-    received = lax.all_to_all(sent, "pages", 0, 0, tiled=False)
-    src_acc = received[:, :share]
-    src_peak = received[:, share, :share]
-    src_total = received[:, share + 1, :share]
-    top = jnp.max(src_peak, axis=0)
-    scale = jnp.exp(src_peak - top[None, :])
-    total = jnp.sum(src_total * scale, axis=0)
-    acc = jnp.sum(src_acc * scale[:, :, None], axis=0)
+    sent = pack_blocks(
+        part[0].reshape(outer_count, inner_count, share),
+        part[1].reshape(outer_count, inner_count, share),
+        part[2].reshape(outer_count, inner_count, share, HEAD_DIM),
+        share,
+    )
+    stage = merge_blocks(lax.all_to_all(sent, "px", 0, 0, tiled=False), share)
+    sent = pack_blocks(*stage, share)
+    top, total, acc = merge_blocks(lax.all_to_all(sent, "pz", 0, 0, tiled=False), share)
     attended_mine = (acc / total[:, None]).astype(jnp.bfloat16)
-    attended = gather_all(attended_mine, "pages")
+    attended = gather_rows(attended_mine)
     flat_heads = attended.reshape(row_count, local_heads * PER_KV * HEAD_DIM)
     head_terms = jnp.dot(flat_heads, w_out, preferred_element_type=jnp.float32)
     mixed_out = jnp.sum(gather_all(head_terms, "kv"), axis=0) + widened
@@ -228,22 +252,28 @@
 
 
 def solution(mesh):
+    row = mesh.devices[0]
+    outer = len({device.coords[0] for device in row})
+    split = Mesh(
+        mesh.devices.reshape(mesh.devices.shape[0], outer, row.size // outer), ("kv", "px", "pz")
+    )
+    pages = ("px", "pz")
     placed = (
         P(),
         P(),
         P(),
         P(),
-        P("kv", "pages"),
-        P("pages"),
-        P("pages", "kv"),
-        P("kv", "pages"),
+        P("kv", pages),
+        P(pages),
+        P(pages, "kv"),
+        P("kv", pages),
         P(None, None, None, "kv"),
-        P(None, "pages", None, "kv"),
+        P(None, pages, None, "kv"),
     )
     return jax.shard_map(
         per_device,
-        mesh=mesh,
+        mesh=split,
         in_specs=placed,
-        out_specs=(P(None, None, "pages"), P(None, None, None, "kv")),
+        out_specs=(P(None, None, pages), P(None, None, None, "kv")),
         check_vma=False,
     )

time: 199 us -> 175 us (0.88)
  blocking collectives: 64.4 us -> 47.5 us
  waiting for transfers between devices: 62.5 us -> 47.4 us
  starting transfers between devices: 40.6 us -> 47.1 us
    all_to_all x1 -> x2, blocking collectives: 36.8 us -> 24.2 us  [the longest x1 14.8 us: per_device(): lax.all_to_all(sent, 'pz', 0, 0, tiled=False)]
    all_to_all x1 -> x2, waiting for transfers between devices: 32.3 us -> 21.2 us  [reduce_rows(): packed = jnp.sum(lax.all_to_all(split, axis, 0, 0, tiled=False), axis=0)]
    all_to_all x3 -> x4, starting transfers between devices: 26.4 us -> 32.5 us  [gather_all(): return lax.all_to_all(spread, axis, 0, 0, tiled=False)]
    all_to_all x1 -> x2, blocking collectives: 27.6 us -> 23.3 us  [gather_all(): return lax.all_to_all(spread, axis, 0, 0, tiled=False)]
    all_to_all x3 -> x4, waiting for transfers between devices: 30.2 us -> 26.2 us  [gather_all(): return lax.all_to_all(spread, axis, 0, 0, tiled=False)]
    unnamed x24 -> x23, local copies, waits for them, and re-layouts: 6.27 us -> 6.95 us
    all_to_all x1 -> x2, starting transfers between devices: 14.2 us -> 14.6 us  [reduce_rows(): packed = jnp.sum(lax.all_to_all(split, axis, 0, 0, tiled=False), axis=0)]
  transfers between devices with their start and end apart: 4 -> 6, of which waited for: 4 -> 6; matrix products, arithmetic and copies ran while one was open for 3% -> 3% of each run, Pallas kernels for 0% -> 0%
where the time goes in v3:
time: 175 us; the launch traced here: 174 us
  blocking collectives  47.5 us (27%)
  waiting for transfers between devices  47.4 us (27%)
  starting transfers between devices  47.1 us (27%)
  local copies, waits for them, and re-layouts  24.3 us (14%)
  other arithmetic  3.69 us (2%)
  matrix products  2.64 us (2%)
    all_to_all x4, starting transfers between devices, gather_all(): return lax.all_to_all(spread, axis, 0, 0, tiled=False)  32.5 us
    all_to_all x4, waiting for transfers between devices, gather_all(): return lax.all_to_all(spread, axis, 0, 0, tiled=False)  26.2 us
    all_to_all x2, blocking collectives, gather_all(): return lax.all_to_all(spread, axis, 0, 0, tiled=False)  23.3 us
    all_to_all x2, waiting for transfers between devices, reduce_rows(): packed = jnp.sum(lax.all_to_all(split, axis, 0, 0, tiled=False), axis=0)  21.2 us
    all_to_all x1, blocking collectives, per_device(): lax.all_to_all(sent, 'pz', 0, 0, tiled=False)  14.8 us
    all_to_all x2, starting transfers between devices, reduce_rows(): packed = jnp.sum(lax.all_to_all(split, axis, 0, 0, tiled=False), axis=0)  14.6 us
    all_to_all x1, blocking collectives, per_device(): stage = merge_blocks(lax.all_to_all(sent, 'px', 0, 0, tiled=False), share)  9.33 us
    unnamed x23, local copies, waits for them, and re-layouts  6.95 us
  transfers between devices with their start and end apart: 6, of which 6 were waited for; matrix products, arithmetic and copies ran while one was open for 3% of the time, Pallas kernels for 0%

profile of v3, /device:TPU:1, one launch (start us, length us, event | category | flops | bytes accessed | tf_op | source)
XLA Modules:
  0.0 173.8 jit_solution(5811439966978405526)
XLA Ops:
  0.7 0.7 copy-done.6
  1.7 1.9 %copy.370 = bf16[4000,112]{1,0:T(8,128)(2,1)S(1)} copy(bf16[4000,112]{0,1:T(8,128)(2,1)} %param.28) | data formatting | bytes 1792000 | tf_op args[4]
  3.6 0.7 gather_fusion.1
  4.5 0.7 broadcast_in_dim.234
  5.3 10.1 %all-to-all-start = ((bf16[8,128,112]{1,2,0:T(8,128)(2,1)}), bf16[8,128,112]{1,2,0:T(8,128)(2,1)S(1)}, u32[]{:S(2)}, u32[]{:S(2)}) async-start(bf16[8,128,112]{1,2,0:T(8,128)(2,1)} %broadcast_in_dim.234), calls=%async_computation | async-start | bytes 458752 | tf_op jit(solution)/shard_map/all_to_all | solution.py:62
  15.4 0.7 copy-done.5
  16.5 0.6 copy-done.8
  17.2 0.6 gather_fusion.2
  17.9 3.7 %all-to-all-done = bf16[8,128,112]{1,2,0:T(8,128)(2,1)S(1)} async-done(((bf16[8,128,112]{1,2,0:T(8,128)(2,1)}), bf16[8,128,112]{1,2,0:T(8,128)(2,1)S(1)}, u32[]{:S(2)}, u32[]{:S(2)}) %all-to-all-start) | async-done | bytes 229408 | tf_op jit(solution)/shard_map/all_to_all | solution.py:62
  22.2 0.9 concatenate.44
  23.2 3.5 %all-to-all-start.1 = ((f32[4,32,1280]{2,1,0:T(8,128)}), f32[4,32,1280]{2,1,0:T(8,128)S(1)}, u32[]{:S(2)}, u32[]{:S(2)}) async-start(f32[4,32,1280]{2,1,0:T(8,128)} %concatenate.44), calls=%async_computation.1 | async-start | bytes 1310720 | tf_op jit(solution)/shard_map/all_to_all | solution.py:76
  26.7 0.6 gather_fusion
  27.4 9.2 %all-to-all-done.1 = f32[4,32,1280]{2,1,0:T(8,128)S(1)} async-done(((f32[4,32,1280]{2,1,0:T(8,128)}), f32[4,32,1280]{2,1,0:T(8,128)S(1)}, u32[]{:S(2)}, u32[]{:S(2)}) %all-to-all-start.1) | async-done | bytes 655392 | tf_op jit(solution)/shard_map/all_to_all | solution.py:76
  36.6 0.8 reshape.1016
  37.4 11.1 %all-to-all-start.2 = ((f32[16,2,1280]{2,1,0:T(2,128)}), f32[16,2,1280]{2,1,0:T(2,128)S(1)}, u32[]{:S(2)}, u32[]{:S(2)}) async-start(f32[16,2,1280]{2,1,0:T(2,128)} %reshape.1016), calls=%async_computation.2 | async-start | bytes 327680 | tf_op jit(solution)/shard_map/all_to_all | solution.py:76
  48.7 11.9 %all-to-all-done.2 = f32[16,2,1280]{2,1,0:T(2,128)S(1)} async-done(((f32[16,2,1280]{2,1,0:T(2,128)}), f32[16,2,1280]{2,1,0:T(2,128)S(1)}, u32[]{:S(2)}, u32[]{:S(2)}) %all-to-all-start.2) | async-done | bytes 163872 | tf_op jit(solution)/shard_map/all_to_all | solution.py:76
  61.1 0.7 broadcast_in_dim.236
  61.8 6.2 %all-to-all-start.3 = ((bf16[16,2,1152]{2,1,0:T(2,128)(2,1)}), bf16[16,2,1152]{2,1,0:T(2,128)(2,1)S(1)}, u32[]{:S(2)}, u32[]{:S(2)}) async-start(bf16[16,2,1152]{2,1,0:T(2,128)(2,1)} %broadcast_in_dim.236), calls=%async_computation.3 | async-start | bytes 147456 | tf_op jit(solution)/shard_map/all_to_all | solution.py:62
  68.1 0.4 copy.384
  68.9 1.6 gather_fusion.5
  70.6 9.1 %all-to-all-done.3 = bf16[16,2,1152]{2,1,0:T(2,128)(2,1)S(1)} async-done(((bf16[16,2,1152]{2,1,0:T(2,128)(2,1)}), bf16[16,2,1152]{2,1,0:T(2,128)(2,1)S(1)}, u32[]{:S(2)}, u32[]{:S(2)}) %all-to-all-start.3) | async-done | bytes 73760 | tf_op jit(solution)/shard_map/all_to_all | solution.py:62
  79.8 0.7 broadcast_in_dim.238
  80.5 3.5 %all-to-all-start.4 = ((bf16[4,32,1152]{2,1,0:T(8,128)(2,1)}), bf16[4,32,1152]{2,1,0:T(8,128)(2,1)S(1)}, u32[]{:S(2)}, u32[]{:S(2)}) async-start(bf16[4,32,1152]{2,1,0:T(8,128)(2,1)} %broadcast_in_dim.238), calls=%async_computation.4 | async-start | bytes 589824 | tf_op jit(solution)/shard_map/all_to_all | solution.py:62
  84.0 5.6 %all-to-all-done.4 = bf16[4,32,1152]{2,1,0:T(8,128)(2,1)S(1)} async-done(((bf16[4,32,1152]{2,1,0:T(8,128)(2,1)}), bf16[4,32,1152]{2,1,0:T(8,128)(2,1)S(1)}, u32[]{:S(2)}, u32[]{:S(2)}) %all-to-all-start.4) | async-done | bytes 294944 | tf_op jit(solution)/shard_map/all_to_all | solution.py:62
  90.0 0.6 gather_fusion.3
  90.8 0.9 copy-done.4
  91.6 0.4 fusion.69
  92.1 0.6 gather_fusion.4
  93.0 1.4 scatter.20
  94.4 0.5 copy.387
  94.9 1.6 gather_fusion.6
  96.7 0.5 fusion.70
  97.2 0.4 fusion.7
  97.5 0.4 fusion.14
  98.1 0.4 fusion.16
  98.5 0.3 convolution_multiply_fusion.1
  99.0 0.4 fusion.12
  101.1 9.3 %all_to_all.50 = f32[4,16,16,128]{3,2,1,0:T(8,128)S(1)} all-to-all(f32[4,16,16,128]{3,2,1,0:T(8,128)S(1)} %pad_maximum_fusion.1), channel_id=1, replica_groups=mesh['kv'=8,'px'=4,'pz'=16] {'px'}, dimensions={0} | all-to-all | bytes 1048576 | tf_op jit(solution)/shard_map/all_to_all | solution.py:243
  110.5 0.4 scatter.29
  111.2 14.8 %all_to_all.51 = f32[16,16,128]{2,1,0:T(8,128)S(1)} all-to-all(f32[16,16,128]{2,1,0:T(8,128)S(1)} %pad_maximum_fusion.2), channel_id=1, replica_groups=mesh['kv'=8,'px'=4,'pz'=16] {'pz'}, dimensions={0} | all-to-all | bytes 262144 | tf_op jit(solution)/shard_map/all_to_all | solution.py:245
  126.3 15.5 %all_to_all.52 = bf16[16,14,128]{2,1,0:T(8,128)(2,1)S(1)} all-to-all(bf16[16,14,128]{2,1,0:T(8,128)(2,1)S(1)} %broadcast_in_dim.252), channel_id=1, replica_groups=mesh['kv'=8,'px'=4,'pz'=16] {'pz'}, dimensions={0} | all-to-all | bytes 114688 | tf_op jit(solution)/shard_map/all_to_all | solution.py:62
  141.8 7.8 %all_to_all.53 = bf16[4,224,128]{2,1,0:T(8,128)(2,1)S(1)} all-to-all(bf16[4,224,128]{2,1,0:T(8,128)(2,1)S(1)} %broadcast_in_dim.254), channel_id=1, replica_groups=mesh['kv'=8,'px'=4,'pz'=16] {'px'}, dimensions={0} | all-to-all | bytes 458752 | tf_op jit(solution)/shard_map/all_to_all | solution.py:62
  149.9 0.7 copy-done.3
  150.8 0.8 broadcast_in_dim.255
  151.6 12.7 %all-to-all-start.9 = ((f32[8,128,112]{1,2,0:T(8,128)}), f32[8,128,112]{1,2,0:T(8,128)S(1)}, u32[]{:S(2)}, u32[]{:S(2)}) async-start(f32[8,128,112]{1,2,0:T(8,128)} %broadcast_in_dim.255), calls=%async_computation.9 | async-start | bytes 917504 | tf_op jit(solution)/shard_map/all_to_all | solution.py:62
  164.3 0.9 copy.406
  165.2 7.8 %all-to-all-done.9 = f32[8,128,112]{1,2,0:T(8,128)S(1)} async-done(((f32[8,128,112]{1,2,0:T(8,128)}), f32[8,128,112]{1,2,0:T(8,128)S(1)}, u32[]{:S(2)}, u32[]{:S(2)}) %all-to-all-start.9) | async-done | bytes 458784 | tf_op jit(solution)/shard_map/all_to_all | solution.py:62
  173.1 0.7 copy.405
  (118 shorter events, 7.1 us)
Async XLA Ops:
  0.6 21.3 %copy-start = (bf16[112,1152]{1,0:T(8,128)(2,1)S(1)}, bf16[112,1152]{1,0:T(8,128)(2,1)}, u32[]{:S(2)}) copy-start(bf16[112,1152]{1,0:T(8,128)(2,1)} %param.30) | copy-start | bytes 774148
  0.7 0.7 copy-start.6
  5.3 16.3 %all-to-all-start = ((bf16[8,128,112]{1,2,0:T(8,128)(2,1)}), bf16[8,128,112]{1,2,0:T(8,128)(2,1)S(1)}, u32[]{:S(2)}, u32[]{:S(2)}) async-start(bf16[8,128,112]{1,2,0:T(8,128)(2,1)} %broadcast_in_dim.234), calls=%async_computation | async-start | bytes 458752 | tf_op jit(solution)/shard_map/all_to_all | solution.py:62
  15.4 0.7 copy-start.5
  15.4 1.8 %copy-start.1 = (s32[8]{0:T(128)S(1)}, s32[8]{0:T(128)}, u32[]{:S(2)}) copy-start(s32[8]{0:T(128)} %param.25) | copy-start | bytes 100
  16.5 0.7 copy-start.8
  23.2 13.4 %all-to-all-start.1 = ((f32[4,32,1280]{2,1,0:T(8,128)}), f32[4,32,1280]{2,1,0:T(8,128)S(1)}, u32[]{:S(2)}, u32[]{:S(2)}) async-start(f32[4,32,1280]{2,1,0:T(8,128)} %concatenate.44), calls=%async_computation.1 | async-start | bytes 1310720 | tf_op jit(solution)/shard_map/all_to_all | solution.py:76
  26.7 0.7 copy-start.7
  37.4 30.7 %copy-start.2 = (bf16[2,64,13,128]{3,1,2,0:T(8,128)(2,1)S(1)}, bf16[2,64,13,128]{3,1,2,0:T(8,128)(2,1)}, u32[]{:S(2)}) copy-start(bf16[2,64,13,128]{3,1,2,0:T(8,128)(2,1)} %param.32) | copy-start | bytes 1277956
  37.4 23.3 %all-to-all-start.2 = ((f32[16,2,1280]{2,1,0:T(2,128)}), f32[16,2,1280]{2,1,0:T(2,128)S(1)}, u32[]{:S(2)}, u32[]{:S(2)}) async-start(f32[16,2,1280]{2,1,0:T(2,128)} %reshape.1016), calls=%async_computation.2 | async-start | bytes 327680 | tf_op jit(solution)/shard_map/all_to_all | solution.py:76
  61.8 17.9 %all-to-all-start.3 = ((bf16[16,2,1152]{2,1,0:T(2,128)(2,1)}), bf16[16,2,1152]{2,1,0:T(2,128)(2,1)S(1)}, u32[]{:S(2)}, u32[]{:S(2)}) async-start(bf16[16,2,1152]{2,1,0:T(2,128)(2,1)} %broadcast_in_dim.236), calls=%async_computation.3 | async-start | bytes 147456 | tf_op jit(solution)/shard_map/all_to_all | solution.py:62
  80.5 9.1 %all-to-all-start.4 = ((bf16[4,32,1152]{2,1,0:T(8,128)(2,1)}), bf16[4,32,1152]{2,1,0:T(8,128)(2,1)S(1)}, u32[]{:S(2)}, u32[]{:S(2)}) async-start(bf16[4,32,1152]{2,1,0:T(8,128)(2,1)} %broadcast_in_dim.238), calls=%async_computation.4 | async-start | bytes 589824 | tf_op jit(solution)/shard_map/all_to_all | solution.py:62
  90.6 1.0 copy-start.4
  149.7 0.9 copy-start.3
  151.6 21.4 %all-to-all-start.9 = ((f32[8,128,112]{1,2,0:T(8,128)}), f32[8,128,112]{1,2,0:T(8,128)S(1)}, u32[]{:S(2)}, u32[]{:S(2)}) async-start(f32[8,128,112]{1,2,0:T(8,128)} %broadcast_in_dim.255), calls=%async_computation.9 | async-start | bytes 917504 | tf_op jit(solution)/shard_map/all_to_all | solution.py:62

commit v4 on v3

--- a/solution.py
+++ b/solution.py
@@ -18,6 +18,7 @@
 THETA = 5000000.0
 EPSILON = 1e-05
 NEGATIVE = -1e30
+STAGES = ("px", "pzh", "pzl")
 
 
 def rotate(values, positions):
@@ -63,14 +64,13 @@
 
 
 def gather_rows(part):
-    inner = gather_all(part, "pz")
-    inner = inner.reshape(-1, *part.shape[1:])
-    outer = gather_all(inner, "px")
-    return outer.reshape(-1, *part.shape[1:])
+    for axis in reversed(STAGES):
+        part = gather_all(part, axis).reshape(-1, *part.shape[1:])
+    return part
 
 
 def reduce_rows(packed):
-    for axis in ("px", "pz"):
+    for axis in STAGES:
         sources = lax.axis_size(axis)
         split = packed.reshape(sources, packed.shape[0] // sources, *packed.shape[1:])
         packed = jnp.sum(lax.all_to_all(split, axis, 0, 0, tiled=False), axis=0)
@@ -98,10 +98,12 @@
 ):
     num_steps, num_seqs = tokens.shape
     row_count = num_steps * num_seqs
-    outer_count = lax.axis_size("px")
-    inner_count = lax.axis_size("pz")
-    page_devices = outer_count * inner_count
-    page_index = lax.axis_index("px") * inner_count + lax.axis_index("pz")
+    stage_sizes = tuple(lax.axis_size(axis) for axis in STAGES)
+    page_devices = 1
+    page_index = 0
+    for axis, size in zip(STAGES, stage_sizes):
+        page_devices = page_devices * size
+        page_index = page_index * size + lax.axis_index(axis)
     local_heads = KV_HEADS // lax.axis_size("kv")
     kv_width = local_heads * HEAD_DIM
     inv_root = 1.0 / jnp.sqrt(jnp.float32(HEAD_DIM))
@@ -235,14 +237,15 @@
     attn_rows = part[0].shape[0]
     share = attn_rows // page_devices
     sent = pack_blocks(
-        part[0].reshape(outer_count, inner_count, share),
-        part[1].reshape(outer_count, inner_count, share),
-        part[2].reshape(outer_count, inner_count, share, HEAD_DIM),
+        part[0].reshape(*stage_sizes, share),
+        part[1].reshape(*stage_sizes, share),
+        part[2].reshape(*stage_sizes, share, HEAD_DIM),
         share,
     )
-    stage = merge_blocks(lax.all_to_all(sent, "px", 0, 0, tiled=False), share)
-    sent = pack_blocks(*stage, share)
-    top, total, acc = merge_blocks(lax.all_to_all(sent, "pz", 0, 0, tiled=False), share)
+    for axis in STAGES:
+        stage = merge_blocks(lax.all_to_all(sent, axis, 0, 0, tiled=False), share)
+        sent = pack_blocks(*stage, share)
+    top, total, acc = stage
     attended_mine = (acc / total[:, None]).astype(jnp.bfloat16)
     attended = gather_rows(attended_mine)
     flat_heads = attended.reshape(row_count, local_heads * PER_KV * HEAD_DIM)
@@ -254,10 +257,13 @@
 def solution(mesh):
     row = mesh.devices[0]
     outer = len({device.coords[0] for device in row})
+    inner = row.size // outer
+    low = 4 if inner % 4 == 0 else inner
     split = Mesh(
-        mesh.devices.reshape(mesh.devices.shape[0], outer, row.size // outer), ("kv", "px", "pz")
-    )
-    pages = ("px", "pz")
+        mesh.devices.reshape(mesh.devices.shape[0], outer, inner // low, low),
+        ("kv",) + STAGES,
+    )
+    pages = STAGES
     placed = (
         P(),
         P(),

time: 175 us -> 211 us (1.21)
  blocking collectives: 47.5 us -> 60.3 us
  starting transfers between devices: 47.1 us -> 59 us
  waiting for transfers between devices: 47.4 us -> 56.5 us
    all_to_all x4 -> x5, starting transfers between devices: 32.5 us -> 40.9 us  [gather_all(): return lax.all_to_all(spread, axis, 0, 0, tiled=False)]
    all_to_all x4 -> x5, waiting for transfers between devices: 26.2 us -> 33.7 us  [gather_all(): return lax.all_to_all(spread, axis, 0, 0, tiled=False)]
    all_to_all x2 -> x3, blocking collectives: 24.2 us -> 31.6 us  [per_device(): stage = merge_blocks(lax.all_to_all(sent, axis, 0, 0, tiled=False), share)]
    all_to_all x2 -> x3, blocking collectives: 23.3 us -> 28.7 us  [gather_all(): return lax.all_to_all(spread, axis, 0, 0, tiled=False)]
    all_to_all x2 -> x3, starting transfers between devices: 14.6 us -> 18.1 us  [reduce_rows(): packed = jnp.sum(lax.all_to_all(split, axis, 0, 0, tiled=False), axis=0)]
    all_to_all x2 -> x3, waiting for transfers between devices: 21.2 us -> 22.8 us  [reduce_rows(): packed = jnp.sum(lax.all_to_all(split, axis, 0, 0, tiled=False), axis=0)]
  transfers between devices with their start and end apart: 6 -> 8, of which waited for: 6 -> 8; matrix products, arithmetic and copies ran while one was open for 3% -> 3% of each run, Pallas kernels for 0% -> 0%
where the time goes in v4:
time: 211 us; the launch traced here: 210 us
  blocking collectives  60.3 us (29%)
  starting transfers between devices  59 us (28%)
  waiting for transfers between devices  56.5 us (27%)
  local copies, waits for them, and re-layouts  25 us (12%)
  other arithmetic  4.91 us (2%)
  matrix products  2.63 us (1%)
    all_to_all x5, starting transfers between devices, gather_all(): return lax.all_to_all(spread, axis, 0, 0, tiled=False)  40.9 us
    all_to_all x5, waiting for transfers between devices, gather_all(): return lax.all_to_all(spread, axis, 0, 0, tiled=False)  33.7 us
    all_to_all x3, blocking collectives, per_device(): stage = merge_blocks(lax.all_to_all(sent, axis, 0, 0, tiled=False), share)  31.6 us
    all_to_all x3, blocking collectives, gather_all(): return lax.all_to_all(spread, axis, 0, 0, tiled=False)  28.7 us
    all_to_all x3, waiting for transfers between devices, reduce_rows(): packed = jnp.sum(lax.all_to_all(split, axis, 0, 0, tiled=False), axis=0)  22.8 us
    all_to_all x3, starting transfers between devices, reduce_rows(): packed = jnp.sum(lax.all_to_all(split, axis, 0, 0, tiled=False), axis=0)  18.1 us
    unnamed x23, local copies, waits for them, and re-layouts  6.93 us
  transfers between devices with their start and end apart: 8, of which 8 were waited for; matrix products, arithmetic and copies ran while one was open for 3% of the time, Pallas kernels for 0%

profile of v4, /device:TPU:1, one launch (start us, length us, event | category | flops | bytes accessed | tf_op | source)
XLA Modules:
  0.0 209.6 jit_solution(14662559218535143133)
XLA Ops:
  0.7 0.7 copy-done.6
  1.7 1.9 copy.353
  3.6 0.7 gather_fusion.1
  4.5 0.7 broadcast_in_dim.251
  5.3 10.1 %all-to-all-start = ((bf16[8,128,112]{1,2,0:T(8,128)(2,1)}), bf16[8,128,112]{1,2,0:T(8,128)(2,1)S(1)}, u32[]{:S(2)}, u32[]{:S(2)}) async-start(bf16[8,128,112]{1,2,0:T(8,128)(2,1)} %broadcast_in_dim.251), calls=%async_computation | async-start | bytes 458752 | tf_op jit(solution)/shard_map/all_to_all | solution.py:63
  15.4 0.7 copy-done.8
  16.3 0.7 copy-done.7
  17.2 4.4 %all-to-all-done = bf16[8,128,112]{1,2,0:T(8,128)(2,1)S(1)} async-done(((bf16[8,128,112]{1,2,0:T(8,128)(2,1)}), bf16[8,128,112]{1,2,0:T(8,128)(2,1)S(1)}, u32[]{:S(2)}, u32[]{:S(2)}) %all-to-all-start) | async-done | bytes 229408 | tf_op jit(solution)/shard_map/all_to_all | solution.py:63
  22.2 0.9 concatenate.52
  23.2 3.6 %all-to-all-start.1 = ((f32[4,32,1280]{2,1,0:T(8,128)}), f32[4,32,1280]{2,1,0:T(8,128)S(1)}, u32[]{:S(2)}, u32[]{:S(2)}) async-start(f32[4,32,1280]{2,1,0:T(8,128)} %concatenate.52), calls=%async_computation.1 | async-start | bytes 1310720 | tf_op jit(solution)/shard_map/all_to_all | solution.py:76
  26.8 0.6 gather_fusion
  27.4 0.6 gather_fusion.2
  28.1 8.6 %all-to-all-done.1 = f32[4,32,1280]{2,1,0:T(8,128)S(1)} async-done(((f32[4,32,1280]{2,1,0:T(8,128)}), f32[4,32,1280]{2,1,0:T(8,128)S(1)}, u32[]{:S(2)}, u32[]{:S(2)}) %all-to-all-start.1) | async-done | bytes 655392 | tf_op jit(solution)/shard_map/all_to_all | solution.py:76
  36.7 0.7 reduce_sum.151
  37.4 10.9 %all-to-all-start.2 = ((f32[4,8,1280]{2,1,0:T(8,128)}), f32[4,8,1280]{2,1,0:T(8,128)S(1)}, u32[]{:S(2)}, u32[]{:S(2)}) async-start(f32[4,8,1280]{2,1,0:T(8,128)} %bitcast.4), calls=%async_computation.2 | async-start | bytes 327680 | tf_op jit(solution)/shard_map/all_to_all | solution.py:76
  49.1 1.6 gather_fusion.5
  50.9 9.7 %all-to-all-done.2 = f32[4,8,1280]{2,1,0:T(8,128)S(1)} async-done(((f32[4,8,1280]{2,1,0:T(8,128)}), f32[4,8,1280]{2,1,0:T(8,128)S(1)}, u32[]{:S(2)}, u32[]{:S(2)}) %all-to-all-start.2) | async-done | bytes 163872 | tf_op jit(solution)/shard_map/all_to_all | solution.py:76
  60.7 0.6 reshape.1117
  61.3 3.6 %all-to-all-start.3 = ((f32[4,2,1280]{2,1,0:T(2,128)}), f32[4,2,1280]{2,1,0:T(2,128)S(1)}, u32[]{:S(2)}, u32[]{:S(2)}) async-start(f32[4,2,1280]{2,1,0:T(2,128)} %reshape.1117), calls=%async_computation.3 | async-start | bytes 81920 | tf_op jit(solution)/shard_map/all_to_all | solution.py:76
  65.0 4.5 %all-to-all-done.3 = f32[4,2,1280]{2,1,0:T(2,128)S(1)} async-done(((f32[4,2,1280]{2,1,0:T(2,128)}), f32[4,2,1280]{2,1,0:T(2,128)S(1)}, u32[]{:S(2)}, u32[]{:S(2)}) %all-to-all-start.3) | async-done | bytes 40992 | tf_op jit(solution)/shard_map/all_to_all | solution.py:76
  69.9 0.6 broadcast_in_dim.253
  70.6 3.3 %all-to-all-start.4 = ((bf16[4,2,1152]{2,1,0:T(2,128)(2,1)}), bf16[4,2,1152]{2,1,0:T(2,128)(2,1)S(1)}, u32[]{:S(2)}, u32[]{:S(2)}) async-start(bf16[4,2,1152]{2,1,0:T(2,128)(2,1)} %broadcast_in_dim.253), calls=%async_computation.4 | async-start | bytes 36864 | tf_op jit(solution)/shard_map/all_to_all | solution.py:63
  73.9 4.3 %all-to-all-done.4 = bf16[4,2,1152]{2,1,0:T(2,128)(2,1)S(1)} async-done(((bf16[4,2,1152]{2,1,0:T(2,128)(2,1)}), bf16[4,2,1152]{2,1,0:T(2,128)(2,1)S(1)}, u32[]{:S(2)}, u32[]{:S(2)}) %all-to-all-start.4) | async-done | bytes 18464 | tf_op jit(solution)/shard_map/all_to_all | solution.py:63
  78.3 0.6 broadcast_in_dim.255
  78.9 4.3 %all-to-all-start.5 = ((bf16[4,8,1152]{2,1,0:T(8,128)(2,1)}), bf16[4,8,1152]{2,1,0:T(8,128)(2,1)S(1)}, u32[]{:S(2)}, u32[]{:S(2)}) async-start(bf16[4,8,1152]{2,1,0:T(8,128)(2,1)} %broadcast_in_dim.255), calls=%async_computation.5 | async-start | bytes 147456 | tf_op jit(solution)/shard_map/all_to_all | solution.py:63
  83.3 11.7 %all-to-all-done.5 = bf16[4,8,1152]{2,1,0:T(8,128)(2,1)S(1)} async-done(((bf16[4,8,1152]{2,1,0:T(8,128)(2,1)}), bf16[4,8,1152]{2,1,0:T(8,128)(2,1)S(1)}, u32[]{:S(2)}, u32[]{:S(2)}) %all-to-all-start.5) | async-done | bytes 73760 | tf_op jit(solution)/shard_map/all_to_all | solution.py:63
  95.0 0.7 broadcast_in_dim.257
  95.7 3.5 %all-to-all-start.6 = ((bf16[4,32,1152]{2,1,0:T(8,128)(2,1)}), bf16[4,32,1152]{2,1,0:T(8,128)(2,1)S(1)}, u32[]{:S(2)}, u32[]{:S(2)}) async-start(bf16[4,32,1152]{2,1,0:T(8,128)(2,1)} %broadcast_in_dim.257), calls=%async_computation.6 | async-start | bytes 589824 | tf_op jit(solution)/shard_map/all_to_all | solution.py:63
  99.3 5.6 %all-to-all-done.6 = bf16[4,32,1152]{2,1,0:T(8,128)(2,1)S(1)} async-done(((bf16[4,32,1152]{2,1,0:T(8,128)(2,1)}), bf16[4,32,1152]{2,1,0:T(8,128)(2,1)S(1)}, u32[]{:S(2)}, u32[]{:S(2)}) %all-to-all-start.6) | async-done | bytes 294944 | tf_op jit(solution)/shard_map/all_to_all | solution.py:63
  105.2 0.6 gather_fusion.3
  106.0 0.9 copy-done.4
  107.3 0.6 gather_fusion.4
  108.3 1.4 scatter.26
  109.6 0.5 copy.370
  110.2 1.6 gather_fusion.6
  115.9 0.5 fusion.13
  116.7 9.5 %all_to_all.70 = f32[4,4,4,16,128]{4,1,3,2,0:T(4,128)S(1)} all-to-all(f32[4,4,4,16,128]{4,1,3,2,0:T(4,128)S(1)} %copy.386), channel_id=1, replica_groups=mesh['kv'=8,'px'=4,'pzh'=4,'pzl'=4] {'px'}, dimensions={0} | all-to-all | bytes 1048576 | tf_op jit(solution)/shard_map/all_to_all | solution.py:246
  127.1 14.7 %all_to_all.71 = f32[4,4,16,128]{3,2,1,0:T(8,128)S(1)} all-to-all(f32[4,4,16,128]{3,2,1,0:T(8,128)S(1)} %copy.390), channel_id=1, replica_groups=mesh['kv'=8,'px'=4,'pzh'=4,'pzl'=4] {'pzh'}, dimensions={0} | all-to-all | bytes 262144 | tf_op jit(solution)/shard_map/all_to_all | solution.py:246
  142.2 7.4 %all_to_all.72 = f32[4,16,128]{2,1,0:T(8,128)S(1)} all-to-all(f32[4,16,128]{2,1,0:T(8,128)S(1)} %pad_maximum_fusion.4), channel_id=1, replica_groups=mesh['kv'=8,'px'=4,'pzh'=4,'pzl'=4] {'pzl'}, dimensions={0} | all-to-all | bytes 65536 | tf_op jit(solution)/shard_map/all_to_all | solution.py:246
  149.8 6.8 %all_to_all.73 = bf16[4,14,128]{2,1,0:T(8,128)(2,1)S(1)} all-to-all(bf16[4,14,128]{2,1,0:T(8,128)(2,1)S(1)} %broadcast_in_dim.271), channel_id=1, replica_groups=mesh['kv'=8,'px'=4,'pzh'=4,'pzl'=4] {'pzl'}, dimensions={0} | all-to-all | bytes 28672 | tf_op jit(solution)/shard_map/all_to_all | solution.py:63
  156.6 14.2 %all_to_all.74 = bf16[4,56,128]{2,1,0:T(8,128)(2,1)S(1)} all-to-all(bf16[4,56,128]{2,1,0:T(8,128)(2,1)S(1)} %broadcast_in_dim.273), channel_id=1, replica_groups=mesh['kv'=8,'px'=4,'pzh'=4,'pzl'=4] {'pzh'}, dimensions={0} | all-to-all | bytes 114688 | tf_op jit(solution)/shard_map/all_to_all | solution.py:63
  170.8 7.7 %all_to_all.75 = bf16[4,224,128]{2,1,0:T(8,128)(2,1)S(1)} all-to-all(bf16[4,224,128]{2,1,0:T(8,128)(2,1)S(1)} %broadcast_in_dim.275), channel_id=1, replica_groups=mesh['kv'=8,'px'=4,'pzh'=4,'pzl'=4] {'px'}, dimensions={0} | all-to-all | bytes 458752 | tf_op jit(solution)/shard_map/all_to_all | solution.py:63
  178.8 0.7 copy-done.3
  179.7 0.8 broadcast_in_dim.276
  180.5 19.7 %all-to-all-start.13 = ((f32[8,128,112]{1,2,0:T(8,128)}), f32[8,128,112]{1,2,0:T(8,128)S(1)}, u32[]{:S(2)}, u32[]{:S(2)}) async-start(f32[8,128,112]{1,2,0:T(8,128)} %broadcast_in_dim.276), calls=%async_computation.13 | async-start | bytes 917504 | tf_op jit(solution)/shard_map/all_to_all | solution.py:63
  200.2 0.9 copy.394
  201.1 7.8 %all-to-all-done.13 = f32[8,128,112]{1,2,0:T(8,128)S(1)} async-done(((f32[8,128,112]{1,2,0:T(8,128)}), f32[8,128,112]{1,2,0:T(8,128)S(1)}, u32[]{:S(2)}, u32[]{:S(2)}) %all-to-all-start.13) | async-done | bytes 458784 | tf_op jit(solution)/shard_map/all_to_all | solution.py:63
  208.9 0.7 copy.393
  (132 shorter events, 10.9 us)
Async XLA Ops:
  0.6 21.3 %copy-start = (bf16[112,1152]{1,0:T(8,128)(2,1)S(1)}, bf16[112,1152]{1,0:T(8,128)(2,1)}, u32[]{:S(2)}) copy-start(bf16[112,1152]{1,0:T(8,128)(2,1)} %param.34) | copy-start | bytes 774148
  0.7 0.7 copy-start.6
  5.3 16.3 %all-to-all-start = ((bf16[8,128,112]{1,2,0:T(8,128)(2,1)}), bf16[8,128,112]{1,2,0:T(8,128)(2,1)S(1)}, u32[]{:S(2)}, u32[]{:S(2)}) async-start(bf16[8,128,112]{1,2,0:T(8,128)(2,1)} %broadcast_in_dim.251), calls=%async_computation | async-start | bytes 458752 | tf_op jit(solution)/shard_map/all_to_all | solution.py:63
  15.4 0.7 copy-start.5
  15.4 0.7 copy-start.8
  16.3 0.7 copy-start.7
  23.2 3.6 %copy-start.1 = (s32[8]{0:T(128)S(1)}, s32[8]{0:T(128)}, u32[]{:S(2)}) copy-start(s32[8]{0:T(128)} %param.29) | copy-start | bytes 100
  23.2 13.6 %all-to-all-start.1 = ((f32[4,32,1280]{2,1,0:T(8,128)}), f32[4,32,1280]{2,1,0:T(8,128)S(1)}, u32[]{:S(2)}, u32[]{:S(2)}) async-start(f32[4,32,1280]{2,1,0:T(8,128)} %concatenate.52), calls=%async_computation.1 | async-start | bytes 1310720 | tf_op jit(solution)/shard_map/all_to_all | solution.py:76
  28.1 20.2 %copy-start.2 = (bf16[2,64,13,128]{3,1,2,0:T(8,128)(2,1)S(1)}, bf16[2,64,13,128]{3,1,2,0:T(8,128)(2,1)}, u32[]{:S(2)}) copy-start(bf16[2,64,13,128]{3,1,2,0:T(8,128)(2,1)} %param.36) | copy-start | bytes 1277956
  37.4 23.2 %all-to-all-start.2 = ((f32[4,8,1280]{2,1,0:T(8,128)}), f32[4,8,1280]{2,1,0:T(8,128)S(1)}, u32[]{:S(2)}, u32[]{:S(2)}) async-start(f32[4,8,1280]{2,1,0:T(8,128)} %bitcast.4), calls=%async_computation.2 | async-start | bytes 327680 | tf_op jit(solution)/shard_map/all_to_all | solution.py:76
  61.3 8.2 %all-to-all-start.3 = ((f32[4,2,1280]{2,1,0:T(2,128)}), f32[4,2,1280]{2,1,0:T(2,128)S(1)}, u32[]{:S(2)}, u32[]{:S(2)}) async-start(f32[4,2,1280]{2,1,0:T(2,128)} %reshape.1117), calls=%async_computation.3 | async-start | bytes 81920 | tf_op jit(solution)/shard_map/all_to_all | solution.py:76
  70.6 7.7 %all-to-all-start.4 = ((bf16[4,2,1152]{2,1,0:T(2,128)(2,1)}), bf16[4,2,1152]{2,1,0:T(2,128)(2,1)S(1)}, u32[]{:S(2)}, u32[]{:S(2)}) async-start(bf16[4,2,1152]{2,1,0:T(2,128)(2,1)} %broadcast_in_dim.253), calls=%async_computation.4 | async-start | bytes 36864 | tf_op jit(solution)/shard_map/all_to_all | solution.py:63
  78.9 16.1 %all-to-all-start.5 = ((bf16[4,8,1152]{2,1,0:T(8,128)(2,1)}), bf16[4,8,1152]{2,1,0:T(8,128)(2,1)S(1)}, u32[]{:S(2)}, u32[]{:S(2)}) async-start(bf16[4,8,1152]{2,1,0:T(8,128)(2,1)} %broadcast_in_dim.255), calls=%async_computation.5 | async-start | bytes 147456 | tf_op jit(solution)/shard_map/all_to_all | solution.py:63
  95.7 9.1 %all-to-all-start.6 = ((bf16[4,32,1152]{2,1,0:T(8,128)(2,1)}), bf16[4,32,1152]{2,1,0:T(8,128)(2,1)S(1)}, u32[]{:S(2)}, u32[]{:S(2)}) async-start(bf16[4,32,1152]{2,1,0:T(8,128)(2,1)} %broadcast_in_dim.257), calls=%async_computation.6 | async-start | bytes 589824 | tf_op jit(solution)/shard_map/all_to_all | solution.py:63
  105.8 1.0 copy-start.4
  178.5 0.9 copy-start.3
  180.5 28.4 %all-to-all-start.13 = ((f32[8,128,112]{1,2,0:T(8,128)}), f32[8,128,112]{1,2,0:T(8,128)S(1)}, u32[]{:S(2)}, u32[]{:S(2)}) async-start(f32[8,128,112]{1,2,0:T(8,128)} %broadcast_in_dim.276), calls=%async_computation.13 | async-start | bytes 917504 | tf_op jit(solution)/shard_map/all_to_all | solution.py:63

commit v5 on v4

--- a/solution.py
+++ b/solution.py
@@ -18,7 +18,7 @@
 THETA = 5000000.0
 EPSILON = 1e-05
 NEGATIVE = -1e30
-STAGES = ("px", "pzh", "pzl")
+STAGES = ("px", "pz")
 
 
 def rotate(values, positions):
@@ -59,8 +59,8 @@
 
 def gather_all(part, axis):
     count = lax.axis_size(axis)
-    spread = jnp.broadcast_to(part[None], (count, *part.shape))
-    return lax.all_to_all(spread, axis, 0, 0, tiled=False)
+    spread = jnp.broadcast_to(part.reshape(1, -1), (count, part.size))
+    return lax.all_to_all(spread, axis, 0, 0, tiled=False).reshape(count, *part.shape)
 
 
 def gather_rows(part):
@@ -72,8 +72,9 @@
 def reduce_rows(packed):
     for axis in STAGES:
         sources = lax.axis_size(axis)
-        split = packed.reshape(sources, packed.shape[0] // sources, *packed.shape[1:])
-        packed = jnp.sum(lax.all_to_all(split, axis, 0, 0, tiled=False), axis=0)
+        block = (packed.shape[0] // sources, *packed.shape[1:])
+        split = packed.reshape(sources, -1)
+        packed = jnp.sum(lax.all_to_all(split, axis, 0, 0, tiled=False), axis=0).reshape(block)
     return packed
 
 
@@ -257,11 +258,8 @@
 def solution(mesh):
     row = mesh.devices[0]
     outer = len({device.coords[0] for device in row})
-    inner = row.size // outer
-    low = 4 if inner % 4 == 0 else inner
     split = Mesh(
-        mesh.devices.reshape(mesh.devices.shape[0], outer, inner // low, low),
-        ("kv",) + STAGES,
+        mesh.devices.reshape(mesh.devices.shape[0], outer, row.size // outer), ("kv",) + STAGES
     )
     pages = STAGES
     placed = (

time: 211 us -> 193 us (0.915)
  other arithmetic: 4.91 us -> 18.7 us
  blocking collectives: 60.3 us -> 47.4 us
  starting transfers between devices: 59 us -> 47.4 us
  waiting for transfers between devices: 56.5 us -> 47.1 us
  local copies, waits for them, and re-layouts: 25 us -> 27.7 us
    all_to_all x8 -> x6, starting transfers between devices: 59 us -> 47.4 us  [the longest x4 32.9 us: gather_all(): lax.all_to_all(spread, axis, 0, 0, tiled=False).reshape(count, *part.shape)]
    all_to_all x8 -> x6, waiting for transfers between devices: 56.5 us -> 47.1 us  [the longest x4 26 us: gather_all(): lax.all_to_all(spread, axis, 0, 0, tiled=False).reshape(count, *part.shape)]
    broadcast_in_dim x0 -> x5, other arithmetic: none -> 8.8 us  [gather_all(): spread = jnp.broadcast_to(part.reshape(1, -1), (count, part.size))]
    all_to_all x3 -> x2, blocking collectives: 31.6 us -> 24.2 us  [per_device(): stage = merge_blocks(lax.all_to_all(sent, axis, 0, 0, tiled=False), share)]
    all_to_all x3 -> x2, blocking collectives: 28.7 us -> 23.2 us  [gather_all(): lax.all_to_all(spread, axis, 0, 0, tiled=False).reshape(count, *part.shape)]
    all_to_all x0 -> x4, other arithmetic: none -> 4.19 us  [gather_all(): lax.all_to_all(spread, axis, 0, 0, tiled=False).reshape(count, *part.shape)]
    unnamed x23 -> x33, local copies, waits for them, and re-layouts: 6.93 us -> 10.7 us
  transfers between devices with their start and end apart: 8 -> 6, of which waited for: 8 -> 6; matrix products, arithmetic and copies ran while one was open for 3% -> 3% of each run, Pallas kernels for 0% -> 0%
where the time goes in v5:
time: 193 us; the launch traced here: 192 us
  starting transfers between devices  47.4 us (25%)
  blocking collectives  47.4 us (25%)
  waiting for transfers between devices  47.1 us (24%)
  local copies, waits for them, and re-layouts  27.7 us (14%)
  other arithmetic  18.7 us (10%)
  matrix products  2.54 us (1%)
    all_to_all x4, starting transfers between devices, gather_all(): lax.all_to_all(spread, axis, 0, 0, tiled=False).reshape(count, *part.shape)  32.9 us
    all_to_all x4, waiting for transfers between devices, gather_all(): lax.all_to_all(spread, axis, 0, 0, tiled=False).reshape(count, *part.shape)  26 us
    all_to_all x2, blocking collectives, per_device(): stage = merge_blocks(lax.all_to_all(sent, axis, 0, 0, tiled=False), share)  24.2 us
    all_to_all x2, blocking collectives, gather_all(): lax.all_to_all(spread, axis, 0, 0, tiled=False).reshape(count, *part.shape)  23.2 us
    all_to_all x2, waiting for transfers between devices, reduce_rows(): lax.all_to_all(split, axis, 0, 0, tiled=False)  21.2 us
    all_to_all x2, starting transfers between devices, reduce_rows(): lax.all_to_all(split, axis, 0, 0, tiled=False)  14.5 us
    unnamed x33, local copies, waits for them, and re-layouts  10.7 us
    broadcast_in_dim x5, other arithmetic, gather_all(): spread = jnp.broadcast_to(part.reshape(1, -1), (count, part.size))  8.8 us
  transfers between devices with their start and end apart: 6, of which 6 were waited for; matrix products, arithmetic and copies ran while one was open for 3% of the time, Pallas kernels for 0%

profile of v5, /device:TPU:1, one launch (start us, length us, event | category | flops | bytes accessed | tf_op | source)
XLA Modules:
  0.0 192.3 jit_solution(16336671444562931324)
XLA Ops:
  0.7 0.7 copy-done.6
  1.7 1.9 %copy.185 = bf16[4000,112]{1,0:T(8,128)(2,1)S(1)} copy(bf16[4000,112]{0,1:T(8,128)(2,1)} %param.28) | data formatting | bytes 1792000 | tf_op args[4]
  3.6 0.7 gather_fusion.1
  4.8 0.5 broadcast.873
  5.3 2.0 %reduce.35 = bf16[8,14336]{1,0:T(8,128)(2,1)S(1)} reduce(bf16[8,1,14336]{2,1,0:T(2,128)(2,1)S(1)} %broadcast_in_dim.235, bf16[]{:T(256)} %broadcast.873), dimensions={1}, to_apply=%broadcast_in_dim.235.reduce_sub_computation | reduce | bytes 458754 | tf_op jit(solution)/shard_map/broadcast_in_dim | solution.py:62
  7.3 0.8 reshape.1167
  8.2 10.3 %all-to-all-start = ((bf16[8,2,7168]{2,1,0:T(2,128)(2,1)}), bf16[8,2,7168]{2,1,0:T(2,128)(2,1)S(1)}, u32[]{:S(2)}, u32[]{:S(2)}) async-start(bf16[8,2,7168]{2,1,0:T(2,128)(2,1)} %reshape.1167), calls=%async_computation | async-start | bytes 458752 | tf_op jit(solution)/shard_map/all_to_all | solution.py:63
  18.5 0.7 copy-done.5
  19.5 0.6 copy-done.8
  20.3 0.6 gather_fusion.2
  20.9 3.7 %all-to-all-done = bf16[8,2,7168]{2,1,0:T(2,128)(2,1)S(1)} async-done(((bf16[8,2,7168]{2,1,0:T(2,128)(2,1)}), bf16[8,2,7168]{2,1,0:T(2,128)(2,1)S(1)}, u32[]{:S(2)}, u32[]{:S(2)}) %all-to-all-start) | async-done | bytes 229408 | tf_op jit(solution)/shard_map/all_to_all | solution.py:63
  25.7 1.5 all_to_all.54
  27.2 3.5 %all-to-all-start.1 = ((f32[4,1,40960]{2,1,0:T(1,128)}), f32[4,1,40960]{2,1,0:T(1,128)S(1)}, u32[]{:S(2)}, u32[]{:S(2)}) async-start(f32[4,1,40960]{2,1,0:T(1,128)} %all_to_all.54), calls=%async_computation.1 | async-start | bytes 1310720 | tf_op jit(solution)/shard_map/all_to_all | solution.py:77
  30.7 0.6 gather_fusion
  31.4 9.2 %all-to-all-done.1 = f32[4,1,40960]{2,1,0:T(1,128)S(1)} async-done(((f32[4,1,40960]{2,1,0:T(1,128)}), f32[4,1,40960]{2,1,0:T(1,128)S(1)}, u32[]{:S(2)}, u32[]{:S(2)}) %all-to-all-start.1) | async-done | bytes 655392 | tf_op jit(solution)/shard_map/all_to_all | solution.py:77
  40.7 1.5 reduce_sum.127
  42.2 11.0 %all-to-all-start.2 = ((f32[16,1,2560]{2,1,0:T(1,128)}), f32[16,1,2560]{2,1,0:T(1,128)S(1)}, u32[]{:S(2)}, u32[]{:S(2)}) async-start(f32[16,1,2560]{2,1,0:T(1,128)} %bitcast.4), calls=%async_computation.2 | async-start | bytes 327680 | tf_op jit(solution)/shard_map/all_to_all | solution.py:77
  53.4 11.9 %all-to-all-done.2 = f32[16,1,2560]{2,1,0:T(1,128)S(1)} async-done(((f32[16,1,2560]{2,1,0:T(1,128)}), f32[16,1,2560]{2,1,0:T(1,128)S(1)}, u32[]{:S(2)}, u32[]{:S(2)}) %all-to-all-start.2) | async-done | bytes 163872 | tf_op jit(solution)/shard_map/all_to_all | solution.py:77
  65.9 1.1 reduce.36
  67.0 0.7 reshape.1169
  67.6 6.2 %all-to-all-start.3 = ((bf16[16,2,1152]{2,1,0:T(2,128)(2,1)}), bf16[16,2,1152]{2,1,0:T(2,128)(2,1)S(1)}, u32[]{:S(2)}, u32[]{:S(2)}) async-start(bf16[16,2,1152]{2,1,0:T(2,128)(2,1)} %reshape.1169), calls=%async_computation.3 | async-start | bytes 147456 | tf_op jit(solution)/shard_map/all_to_all | solution.py:63
  74.8 1.6 gather_fusion.5
  76.5 9.1 %all-to-all-done.3 = bf16[16,2,1152]{2,1,0:T(2,128)(2,1)S(1)} async-done(((bf16[16,2,1152]{2,1,0:T(2,128)(2,1)}), bf16[16,2,1152]{2,1,0:T(2,128)(2,1)S(1)}, u32[]{:S(2)}, u32[]{:S(2)}) %all-to-all-start.3) | async-done | bytes 73760 | tf_op jit(solution)/shard_map/all_to_all | solution.py:63
  86.5 2.6 %reduce.37 = bf16[4,36864]{1,0:T(4,128)(2,1)S(1)} reduce(bf16[4,1,36864]{2,1,0:T(2,128)(2,1)S(1)} %broadcast_in_dim.240, bf16[]{:T(256)} %broadcast.873), dimensions={1}, to_apply=%broadcast_in_dim.240.reduce_sub_computation | reduce | bytes 589826 | tf_op jit(solution)/shard_map/broadcast_in_dim | solution.py:62
  89.1 1.0 reshape.1171
  90.1 3.7 %all-to-all-start.4 = ((bf16[4,2,18432]{2,1,0:T(2,128)(2,1)}), bf16[4,2,18432]{2,1,0:T(2,128)(2,1)S(1)}, u32[]{:S(2)}, u32[]{:S(2)}) async-start(bf16[4,2,18432]{2,1,0:T(2,128)(2,1)} %reshape.1171), calls=%async_computation.4 | async-start | bytes 589824 | tf_op jit(solution)/shard_map/all_to_all | solution.py:63
  93.9 5.4 %all-to-all-done.4 = bf16[4,2,18432]{2,1,0:T(2,128)(2,1)S(1)} async-done(((bf16[4,2,18432]{2,1,0:T(2,128)(2,1)}), bf16[4,2,18432]{2,1,0:T(2,128)(2,1)S(1)}, u32[]{:S(2)}, u32[]{:S(2)}) %all-to-all-start.4) | async-done | bytes 294944 | tf_op jit(solution)/shard_map/all_to_all | solution.py:63
  99.6 2.0 %reduce.31 = bf16[4,36864]{1,0:T(4,128)(2,1)S(1)} reduce(bf16[4,1,36864]{2,1,0:T(2,128)(2,1)S(1)} %reshape.1172, bf16[]{:T(256)} %constant.354), dimensions={1}, to_apply=%all_to_all.48.reduce_sub_computation | reduce | bytes 589826 | tf_op jit(solution)/shard_map/all_to_all | solution.py:63
  102.0 0.6 gather_fusion.3
  102.8 0.9 copy-done.4
  104.1 0.6 gather_fusion.4
  105.1 1.4 scatter.20
  106.4 0.5 copy.201
  106.9 1.6 gather_fusion.6
  108.8 0.5 fusion.71
  113.1 9.3 %all_to_all.65 = f32[4,16,16,128]{3,2,1,0:T(8,128)S(1)} all-to-all(f32[4,16,16,128]{3,2,1,0:T(8,128)S(1)} %pad_maximum_fusion.1), channel_id=1, replica_groups=mesh['kv'=8,'px'=4,'pz'=16] {'px'}, dimensions={0} | all-to-all | bytes 1048576 | tf_op jit(solution)/shard_map/all_to_all | solution.py:247
  123.2 14.8 %all_to_all.66 = f32[16,16,128]{2,1,0:T(8,128)S(1)} all-to-all(f32[16,16,128]{2,1,0:T(8,128)S(1)} %pad_maximum_fusion.2), channel_id=1, replica_groups=mesh['kv'=8,'px'=4,'pz'=16] {'pz'}, dimensions={0} | all-to-all | bytes 262144 | tf_op jit(solution)/shard_map/all_to_all | solution.py:247
  138.4 1.0 reduce.38
  139.4 15.5 %all_to_all.67 = bf16[16,2,896]{2,1,0:T(2,128)(2,1)S(1)} all-to-all(bf16[16,2,896]{2,1,0:T(2,128)(2,1)S(1)} %reshape.1173), channel_id=1, replica_groups=mesh['kv'=8,'px'=4,'pz'=16] {'pz'}, dimensions={0} | all-to-all | bytes 114688 | tf_op jit(solution)/shard_map/all_to_all | solution.py:63
  155.6 2.2 %reduce.39 = bf16[4,28672]{1,0:T(4,128)(2,1)S(1)} reduce(bf16[4,1,28672]{2,1,0:T(2,128)(2,1)S(1)} %broadcast_in_dim.256, bf16[]{:T(256)} %broadcast.873), dimensions={1}, to_apply=%broadcast_in_dim.256.reduce_sub_computation | reduce | bytes 458754 | tf_op jit(solution)/shard_map/broadcast_in_dim | solution.py:62
  158.0 7.7 %all_to_all.68 = bf16[4,2,14336]{2,1,0:T(2,128)(2,1)S(1)} all-to-all(bf16[4,2,14336]{2,1,0:T(2,128)(2,1)S(1)} %reshape.1175), channel_id=1, replica_groups=mesh['kv'=8,'px'=4,'pz'=16] {'px'}, dimensions={0} | all-to-all | bytes 458752 | tf_op jit(solution)/shard_map/all_to_all | solution.py:63
  166.0 1.5 reduce.33
  167.6 0.8 copy-done.3
  168.7 1.0 broadcast_in_dim.258
  169.7 12.8 %all-to-all-start.9 = ((f32[8,1,14336]{2,1,0:T(1,128)}), f32[8,1,14336]{2,1,0:T(1,128)S(1)}, u32[]{:S(2)}, u32[]{:S(2)}) async-start(f32[8,1,14336]{2,1,0:T(1,128)} %broadcast_in_dim.258), calls=%async_computation.9 | async-start | bytes 917504 | tf_op jit(solution)/shard_map/all_to_all | solution.py:63
  182.5 0.9 copy.221
  183.4 7.8 %all-to-all-done.9 = f32[8,1,14336]{2,1,0:T(1,128)S(1)} async-done(((f32[8,1,14336]{2,1,0:T(1,128)}), f32[8,1,14336]{2,1,0:T(1,128)S(1)}, u32[]{:S(2)}, u32[]{:S(2)}) %all-to-all-start.9) | async-done | bytes 458784 | tf_op jit(solution)/shard_map/all_to_all | solution.py:63
  191.6 0.7 convert_element_type.64
  (139 shorter events, 13.8 us)
Async XLA Ops:
  0.6 24.8 %copy-start = (bf16[112,1152]{1,0:T(8,128)(2,1)S(1)}, bf16[112,1152]{1,0:T(8,128)(2,1)}, u32[]{:S(2)}) copy-start(bf16[112,1152]{1,0:T(8,128)(2,1)} %param.30) | copy-start | bytes 774148
  0.7 0.7 copy-start.6
  8.2 12.1 %copy-start.1 = (s32[8]{0:T(128)S(1)}, s32[8]{0:T(128)}, u32[]{:S(2)}) copy-start(s32[8]{0:T(128)} %param.25) | copy-start | bytes 100
  8.2 16.5 %all-to-all-start = ((bf16[8,2,7168]{2,1,0:T(2,128)(2,1)}), bf16[8,2,7168]{2,1,0:T(2,128)(2,1)S(1)}, u32[]{:S(2)}, u32[]{:S(2)}) async-start(bf16[8,2,7168]{2,1,0:T(2,128)(2,1)} %reshape.1167), calls=%async_computation | async-start | bytes 458752 | tf_op jit(solution)/shard_map/all_to_all | solution.py:63
  18.5 0.7 copy-start.5
  19.5 0.7 copy-start.8
  27.2 13.4 %all-to-all-start.1 = ((f32[4,1,40960]{2,1,0:T(1,128)}), f32[4,1,40960]{2,1,0:T(1,128)S(1)}, u32[]{:S(2)}, u32[]{:S(2)}) async-start(f32[4,1,40960]{2,1,0:T(1,128)} %all_to_all.54), calls=%async_computation.1 | async-start | bytes 1310720 | tf_op jit(solution)/shard_map/all_to_all | solution.py:77
  30.7 0.7 copy-start.7
  42.2 23.1 %all-to-all-start.2 = ((f32[16,1,2560]{2,1,0:T(1,128)}), f32[16,1,2560]{2,1,0:T(1,128)S(1)}, u32[]{:S(2)}, u32[]{:S(2)}) async-start(f32[16,1,2560]{2,1,0:T(1,128)} %bitcast.4), calls=%async_computation.2 | async-start | bytes 327680 | tf_op jit(solution)/shard_map/all_to_all | solution.py:77
  65.4 8.5 %copy-start.2 = (bf16[2,64,13,128]{3,1,2,0:T(8,128)(2,1)S(1)}, bf16[2,64,13,128]{3,1,2,0:T(8,128)(2,1)}, u32[]{:S(2)}) copy-start(bf16[2,64,13,128]{3,1,2,0:T(8,128)(2,1)} %param.32) | copy-start | bytes 1277956
  67.6 17.9 %all-to-all-start.3 = ((bf16[16,2,1152]{2,1,0:T(2,128)(2,1)}), bf16[16,2,1152]{2,1,0:T(2,128)(2,1)S(1)}, u32[]{:S(2)}, u32[]{:S(2)}) async-start(bf16[16,2,1152]{2,1,0:T(2,128)(2,1)} %reshape.1169), calls=%async_computation.3 | async-start | bytes 147456 | tf_op jit(solution)/shard_map/all_to_all | solution.py:63
  90.1 9.1 %all-to-all-start.4 = ((bf16[4,2,18432]{2,1,0:T(2,128)(2,1)}), bf16[4,2,18432]{2,1,0:T(2,128)(2,1)S(1)}, u32[]{:S(2)}, u32[]{:S(2)}) async-start(bf16[4,2,18432]{2,1,0:T(2,128)(2,1)} %reshape.1171), calls=%async_computation.4 | async-start | bytes 589824 | tf_op jit(solution)/shard_map/all_to_all | solution.py:63
  102.6 1.0 copy-start.4
  167.5 0.9 copy-start.3
  169.7 21.5 %all-to-all-start.9 = ((f32[8,1,14336]{2,1,0:T(1,128)}), f32[8,1,14336]{2,1,0:T(1,128)S(1)}, u32[]{:S(2)}, u32[]{:S(2)}) async-start(f32[8,1,14336]{2,1,0:T(1,128)} %broadcast_in_dim.258), calls=%async_computation.9 | async-start | bytes 917504 | tf_op jit(solution)/shard_map/all_to_all | solution.py:63

commit v6 on v3

--- a/solution.py
+++ b/solution.py
@@ -247,7 +247,8 @@
     attended = gather_rows(attended_mine)
     flat_heads = attended.reshape(row_count, local_heads * PER_KV * HEAD_DIM)
     head_terms = jnp.dot(flat_heads, w_out, preferred_element_type=jnp.float32)
-    mixed_out = jnp.sum(gather_all(head_terms, "kv"), axis=0) + widened
+    shared = gather_all(head_terms.astype(jnp.bfloat16), "kv").astype(jnp.float32)
+    mixed_out = jnp.sum(shared, axis=0) + widened
     return (mixed_out.astype(jnp.bfloat16).reshape(num_steps, num_seqs, -1), buffer)
 
 

time: 175 us -> 172 us (0.983)
  waiting for transfers between devices: 47.4 us -> 44.9 us
    all_to_all x4, waiting for transfers between devices: 26.2 us -> 23.7 us  [gather_all(): return lax.all_to_all(spread, axis, 0, 0, tiled=False)]
where the time goes in v6:
time: 172 us; the launch traced here: 171 us
  blocking collectives  47.5 us (28%)
  starting transfers between devices  47 us (27%)
  waiting for transfers between devices  44.9 us (26%)
  local copies, waits for them, and re-layouts  24.2 us (14%)
  other arithmetic  3.69 us (2%)
  matrix products  2.65 us (2%)
    all_to_all x4, starting transfers between devices, gather_all(): return lax.all_to_all(spread, axis, 0, 0, tiled=False)  32.4 us
    all_to_all x4, waiting for transfers between devices, gather_all(): return lax.all_to_all(spread, axis, 0, 0, tiled=False)  23.7 us
    all_to_all x2, blocking collectives, gather_all(): return lax.all_to_all(spread, axis, 0, 0, tiled=False)  23.3 us
    all_to_all x2, waiting for transfers between devices, reduce_rows(): packed = jnp.sum(lax.all_to_all(split, axis, 0, 0, tiled=False), axis=0)  21.2 us
    all_to_all x1, blocking collectives, per_device(): lax.all_to_all(sent, 'pz', 0, 0, tiled=False)  14.8 us
    all_to_all x2, starting transfers between devices, reduce_rows(): packed = jnp.sum(lax.all_to_all(split, axis, 0, 0, tiled=False), axis=0)  14.6 us
    all_to_all x1, blocking collectives, per_device(): stage = merge_blocks(lax.all_to_all(sent, 'px', 0, 0, tiled=False), share)  9.33 us
    unnamed x23, local copies, waits for them, and re-layouts  6.95 us
  transfers between devices with their start and end apart: 6, of which 6 were waited for; matrix products, arithmetic and copies ran while one was open for 3% of the time, Pallas kernels for 0%

profile of v6, /device:TPU:1, one launch (start us, length us, event | category | flops | bytes accessed | tf_op | source)
XLA Modules:
  0.0 171.1 jit_solution(15977944117416236768)
XLA Ops:
  0.7 0.7 copy-done.6
  1.7 1.9 %copy.370 = bf16[4000,112]{1,0:T(8,128)(2,1)S(1)} copy(bf16[4000,112]{0,1:T(8,128)(2,1)} %param.28) | data formatting | bytes 1792000 | tf_op args[4]
  3.6 0.7 gather_fusion.1
  4.5 0.7 broadcast_in_dim.234
  5.3 10.1 %all-to-all-start = ((bf16[8,128,112]{1,2,0:T(8,128)(2,1)}), bf16[8,128,112]{1,2,0:T(8,128)(2,1)S(1)}, u32[]{:S(2)}, u32[]{:S(2)}) async-start(bf16[8,128,112]{1,2,0:T(8,128)(2,1)} %broadcast_in_dim.234), calls=%async_computation | async-start | bytes 458752 | tf_op jit(solution)/shard_map/all_to_all | solution.py:62
  15.4 0.7 copy-done.5
  16.5 0.6 copy-done.8
  17.2 0.6 gather_fusion.2
  17.9 3.7 %all-to-all-done = bf16[8,128,112]{1,2,0:T(8,128)(2,1)S(1)} async-done(((bf16[8,128,112]{1,2,0:T(8,128)(2,1)}), bf16[8,128,112]{1,2,0:T(8,128)(2,1)S(1)}, u32[]{:S(2)}, u32[]{:S(2)}) %all-to-all-start) | async-done | bytes 229408 | tf_op jit(solution)/shard_map/all_to_all | solution.py:62
  22.2 0.9 concatenate.44
  23.2 3.5 %all-to-all-start.1 = ((f32[4,32,1280]{2,1,0:T(8,128)}), f32[4,32,1280]{2,1,0:T(8,128)S(1)}, u32[]{:S(2)}, u32[]{:S(2)}) async-start(f32[4,32,1280]{2,1,0:T(8,128)} %concatenate.44), calls=%async_computation.1 | async-start | bytes 1310720 | tf_op jit(solution)/shard_map/all_to_all | solution.py:76
  26.7 0.6 gather_fusion
  27.4 9.2 %all-to-all-done.1 = f32[4,32,1280]{2,1,0:T(8,128)S(1)} async-done(((f32[4,32,1280]{2,1,0:T(8,128)}), f32[4,32,1280]{2,1,0:T(8,128)S(1)}, u32[]{:S(2)}, u32[]{:S(2)}) %all-to-all-start.1) | async-done | bytes 655392 | tf_op jit(solution)/shard_map/all_to_all | solution.py:76
  36.6 0.8 reshape.1016
  37.4 11.1 %all-to-all-start.2 = ((f32[16,2,1280]{2,1,0:T(2,128)}), f32[16,2,1280]{2,1,0:T(2,128)S(1)}, u32[]{:S(2)}, u32[]{:S(2)}) async-start(f32[16,2,1280]{2,1,0:T(2,128)} %reshape.1016), calls=%async_computation.2 | async-start | bytes 327680 | tf_op jit(solution)/shard_map/all_to_all | solution.py:76
  48.7 11.9 %all-to-all-done.2 = f32[16,2,1280]{2,1,0:T(2,128)S(1)} async-done(((f32[16,2,1280]{2,1,0:T(2,128)}), f32[16,2,1280]{2,1,0:T(2,128)S(1)}, u32[]{:S(2)}, u32[]{:S(2)}) %all-to-all-start.2) | async-done | bytes 163872 | tf_op jit(solution)/shard_map/all_to_all | solution.py:76
  61.1 0.7 broadcast_in_dim.236
  61.8 6.2 %all-to-all-start.3 = ((bf16[16,2,1152]{2,1,0:T(2,128)(2,1)}), bf16[16,2,1152]{2,1,0:T(2,128)(2,1)S(1)}, u32[]{:S(2)}, u32[]{:S(2)}) async-start(bf16[16,2,1152]{2,1,0:T(2,128)(2,1)} %broadcast_in_dim.236), calls=%async_computation.3 | async-start | bytes 147456 | tf_op jit(solution)/shard_map/all_to_all | solution.py:62
  68.1 0.4 copy.384
  68.9 1.6 gather_fusion.5
  70.6 9.1 %all-to-all-done.3 = bf16[16,2,1152]{2,1,0:T(2,128)(2,1)S(1)} async-done(((bf16[16,2,1152]{2,1,0:T(2,128)(2,1)}), bf16[16,2,1152]{2,1,0:T(2,128)(2,1)S(1)}, u32[]{:S(2)}, u32[]{:S(2)}) %all-to-all-start.3) | async-done | bytes 73760 | tf_op jit(solution)/shard_map/all_to_all | solution.py:62
  79.8 0.7 broadcast_in_dim.238
  80.5 3.5 %all-to-all-start.4 = ((bf16[4,32,1152]{2,1,0:T(8,128)(2,1)}), bf16[4,32,1152]{2,1,0:T(8,128)(2,1)S(1)}, u32[]{:S(2)}, u32[]{:S(2)}) async-start(bf16[4,32,1152]{2,1,0:T(8,128)(2,1)} %broadcast_in_dim.238), calls=%async_computation.4 | async-start | bytes 589824 | tf_op jit(solution)/shard_map/all_to_all | solution.py:62
  84.0 5.6 %all-to-all-done.4 = bf16[4,32,1152]{2,1,0:T(8,128)(2,1)S(1)} async-done(((bf16[4,32,1152]{2,1,0:T(8,128)(2,1)}), bf16[4,32,1152]{2,1,0:T(8,128)(2,1)S(1)}, u32[]{:S(2)}, u32[]{:S(2)}) %all-to-all-start.4) | async-done | bytes 294944 | tf_op jit(solution)/shard_map/all_to_all | solution.py:62
  90.0 0.6 gather_fusion.3
  90.8 0.9 copy-done.4
  91.6 0.4 fusion.69
  92.1 0.6 gather_fusion.4
  93.0 1.4 scatter.20
  94.4 0.5 copy.387
  94.9 1.6 gather_fusion.6
  96.7 0.5 fusion.70
  97.2 0.3 fusion.7
  97.5 0.4 fusion.14
  98.1 0.4 fusion.16
  98.5 0.3 convolution_multiply_fusion.1
  99.0 0.5 fusion.12
  101.1 9.3 %all_to_all.50 = f32[4,16,16,128]{3,2,1,0:T(8,128)S(1)} all-to-all(f32[4,16,16,128]{3,2,1,0:T(8,128)S(1)} %pad_maximum_fusion.1), channel_id=1, replica_groups=mesh['kv'=8,'px'=4,'pz'=16] {'px'}, dimensions={0} | all-to-all | bytes 1048576 | tf_op jit(solution)/shard_map/all_to_all | solution.py:243
  110.5 0.4 scatter.29
  111.2 14.8 %all_to_all.51 = f32[16,16,128]{2,1,0:T(8,128)S(1)} all-to-all(f32[16,16,128]{2,1,0:T(8,128)S(1)} %pad_maximum_fusion.2), channel_id=1, replica_groups=mesh['kv'=8,'px'=4,'pz'=16] {'pz'}, dimensions={0} | all-to-all | bytes 262144 | tf_op jit(solution)/shard_map/all_to_all | solution.py:245
  126.3 15.5 %all_to_all.52 = bf16[16,14,128]{2,1,0:T(8,128)(2,1)S(1)} all-to-all(bf16[16,14,128]{2,1,0:T(8,128)(2,1)S(1)} %broadcast_in_dim.252), channel_id=1, replica_groups=mesh['kv'=8,'px'=4,'pz'=16] {'pz'}, dimensions={0} | all-to-all | bytes 114688 | tf_op jit(solution)/shard_map/all_to_all | solution.py:62
  141.8 7.8 %all_to_all.53 = bf16[4,224,128]{2,1,0:T(8,128)(2,1)S(1)} all-to-all(bf16[4,224,128]{2,1,0:T(8,128)(2,1)S(1)} %broadcast_in_dim.254), channel_id=1, replica_groups=mesh['kv'=8,'px'=4,'pz'=16] {'px'}, dimensions={0} | all-to-all | bytes 458752 | tf_op jit(solution)/shard_map/all_to_all | solution.py:62
  149.9 0.7 copy-done.3
  150.8 0.7 broadcast_in_dim.255
  151.5 12.6 %all-to-all-start.9 = ((bf16[8,128,112]{1,2,0:T(8,128)(2,1)}), bf16[8,128,112]{1,2,0:T(8,128)(2,1)S(1)}, u32[]{:S(2)}, u32[]{:S(2)}) async-start(bf16[8,128,112]{1,2,0:T(8,128)(2,1)} %broadcast_in_dim.255), calls=%async_computation.9 | async-start | bytes 458752 | tf_op jit(solution)/shard_map/all_to_all | solution.py:62
  164.2 0.9 copy.406
  165.1 5.3 %all-to-all-done.9 = bf16[8,128,112]{1,2,0:T(8,128)(2,1)S(1)} async-done(((bf16[8,128,112]{1,2,0:T(8,128)(2,1)}), bf16[8,128,112]{1,2,0:T(8,128)(2,1)S(1)}, u32[]{:S(2)}, u32[]{:S(2)}) %all-to-all-start.9) | async-done | bytes 229408 | tf_op jit(solution)/shard_map/all_to_all | solution.py:62
  170.4 0.7 copy.405
  (118 shorter events, 7.1 us)
Async XLA Ops:
  0.6 21.3 %copy-start = (bf16[112,1152]{1,0:T(8,128)(2,1)S(1)}, bf16[112,1152]{1,0:T(8,128)(2,1)}, u32[]{:S(2)}) copy-start(bf16[112,1152]{1,0:T(8,128)(2,1)} %param.30) | copy-start | bytes 774148
  0.7 0.7 copy-start.6
  5.3 16.3 %all-to-all-start = ((bf16[8,128,112]{1,2,0:T(8,128)(2,1)}), bf16[8,128,112]{1,2,0:T(8,128)(2,1)S(1)}, u32[]{:S(2)}, u32[]{:S(2)}) async-start(bf16[8,128,112]{1,2,0:T(8,128)(2,1)} %broadcast_in_dim.234), calls=%async_computation | async-start | bytes 458752 | tf_op jit(solution)/shard_map/all_to_all | solution.py:62
  15.4 0.7 copy-start.5
  15.4 1.8 %copy-start.1 = (s32[8]{0:T(128)S(1)}, s32[8]{0:T(128)}, u32[]{:S(2)}) copy-start(s32[8]{0:T(128)} %param.25) | copy-start | bytes 100
  16.5 0.7 copy-start.8
  23.2 13.4 %all-to-all-start.1 = ((f32[4,32,1280]{2,1,0:T(8,128)}), f32[4,32,1280]{2,1,0:T(8,128)S(1)}, u32[]{:S(2)}, u32[]{:S(2)}) async-start(f32[4,32,1280]{2,1,0:T(8,128)} %concatenate.44), calls=%async_computation.1 | async-start | bytes 1310720 | tf_op jit(solution)/shard_map/all_to_all | solution.py:76
  26.7 0.7 copy-start.7
  37.4 30.7 %copy-start.2 = (bf16[2,64,13,128]{3,1,2,0:T(8,128)(2,1)S(1)}, bf16[2,64,13,128]{3,1,2,0:T(8,128)(2,1)}, u32[]{:S(2)}) copy-start(bf16[2,64,13,128]{3,1,2,0:T(8,128)(2,1)} %param.32) | copy-start | bytes 1277956
  37.4 23.3 %all-to-all-start.2 = ((f32[16,2,1280]{2,1,0:T(2,128)}), f32[16,2,1280]{2,1,0:T(2,128)S(1)}, u32[]{:S(2)}, u32[]{:S(2)}) async-start(f32[16,2,1280]{2,1,0:T(2,128)} %reshape.1016), calls=%async_computation.2 | async-start | bytes 327680 | tf_op jit(solution)/shard_map/all_to_all | solution.py:76
  61.8 17.9 %all-to-all-start.3 = ((bf16[16,2,1152]{2,1,0:T(2,128)(2,1)}), bf16[16,2,1152]{2,1,0:T(2,128)(2,1)S(1)}, u32[]{:S(2)}, u32[]{:S(2)}) async-start(bf16[16,2,1152]{2,1,0:T(2,128)(2,1)} %broadcast_in_dim.236), calls=%async_computation.3 | async-start | bytes 147456 | tf_op jit(solution)/shard_map/all_to_all | solution.py:62
  80.5 9.1 %all-to-all-start.4 = ((bf16[4,32,1152]{2,1,0:T(8,128)(2,1)}), bf16[4,32,1152]{2,1,0:T(8,128)(2,1)S(1)}, u32[]{:S(2)}, u32[]{:S(2)}) async-start(bf16[4,32,1152]{2,1,0:T(8,128)(2,1)} %broadcast_in_dim.238), calls=%async_computation.4 | async-start | bytes 589824 | tf_op jit(solution)/shard_map/all_to_all | solution.py:62
  90.6 1.0 copy-start.4
  149.7 0.9 copy-start.3
  151.5 18.8 %all-to-all-start.9 = ((bf16[8,128,112]{1,2,0:T(8,128)(2,1)}), bf16[8,128,112]{1,2,0:T(8,128)(2,1)S(1)}, u32[]{:S(2)}, u32[]{:S(2)}) async-start(bf16[8,128,112]{1,2,0:T(8,128)(2,1)} %broadcast_in_dim.255), calls=%async_computation.9 | async-start | bytes 458752 | tf_op jit(solution)/shard_map/all_to_all | solution.py:62

commit v7 on v6

--- a/solution.py
+++ b/solution.py
@@ -87,9 +87,8 @@
 
 
 def pack_blocks(top, total, acc, share):
-    stats = jnp.zeros((*acc.shape[:-2], 2, HEAD_DIM), jnp.float32)
-    stats = stats.at[..., 0, :share].set(top)
-    stats = stats.at[..., 1, :share].set(total)
+    widths = [(0, 0)] * (top.ndim - 1) + [(0, HEAD_DIM - share)]
+    stats = jnp.stack([jnp.pad(top, widths), jnp.pad(total, widths)], axis=-2)
     return jnp.concatenate([acc, stats], axis=-2)
 
 
@@ -107,9 +106,10 @@
     inv_root = 1.0 / jnp.sqrt(jnp.float32(HEAD_DIM))
     vocab_local = embedding.shape[0]
     local_ids = tokens.reshape(-1) - lax.axis_index("kv") * vocab_local
-    inside = (local_ids >= 0) & (local_ids < vocab_local)
-    picked = jnp.take(embedding, jnp.clip(local_ids, 0, vocab_local - 1), axis=0)
-    found = jnp.where(inside[:, None], picked, jnp.zeros_like(picked))
+    pick = local_ids[:, None] == jnp.arange(vocab_local, dtype=jnp.int32)[None, :]
+    found = jnp.dot(
+        pick.astype(jnp.bfloat16), embedding, preferred_element_type=jnp.float32
+    ).astype(jnp.bfloat16)
     widened = jnp.sum(gather_all(found, "kv").astype(jnp.float32), axis=0)
     squares = jnp.sum(widened * widened, axis=1)
     normed = (widened * norm_gain.astype(jnp.float32)).astype(jnp.bfloat16)
@@ -136,8 +136,16 @@
     )
     snapshots = []
     for step_index in range(num_steps):
-        buffer = jnp.take(buffer, parents[step_index], axis=1)
-        buffer = buffer.at[:, :, PRIOR + step_index].set(fresh_kv[:, step_index])
+        choose = parents[step_index][:, None] == jnp.arange(num_seqs, dtype=jnp.int32)[None, :]
+        buffer = jnp.einsum(
+            "nb,kbld->knld",
+            choose.astype(jnp.bfloat16),
+            buffer,
+            preferred_element_type=jnp.float32,
+        ).astype(jnp.bfloat16)
+        buffer = lax.dynamic_update_slice(
+            buffer, fresh_kv[:, step_index][:, :, None, :], (0, 0, PRIOR + step_index, 0)
+        )
         snapshots.append(buffer)
     stacked = jnp.stack(snapshots)
     tail_keys = stacked[:, 0].reshape(num_steps, num_seqs, HISTORY, local_heads, HEAD_DIM)

time: 172 us -> 163 us (0.948)
  blocking collectives: 47.5 us -> 65.4 us
  local copies, waits for them, and re-layouts: 24.2 us -> 10.2 us
  starting transfers between devices: 47 us -> 34.4 us
  waiting for transfers between devices: 44.9 us -> 43.1 us
    all_to_all x2 -> x3, blocking collectives: 23.3 us -> 41.2 us  [gather_all(): return lax.all_to_all(spread, axis, 0, 0, tiled=False)]
    all_to_all x4 -> x3, starting transfers between devices: 32.4 us -> 19.8 us  [gather_all(): return lax.all_to_all(spread, axis, 0, 0, tiled=False)]
    unnamed x23 -> x22, local copies, waits for them, and re-layouts: 6.95 us -> 1.29 us
    gather x3 -> x0, local copies, waits for them, and re-layouts: 3.82 us -> none  [the longest x2 3.11 us: per_device(): buffer = jnp.take(buffer, parents[step_index], axis=1)]
    scatter x7 -> x0, local copies, waits for them, and re-layouts: 2.62 us -> none  [the longest x3 1.98 us: per_device(): buffer = buffer.at[:, :, PRIOR + step_index].set(fresh_kv[:, step_index])]
    all_to_all x4 -> x3, waiting for transfers between devices: 23.7 us -> 22.6 us  [gather_all(): return lax.all_to_all(spread, axis, 0, 0, tiled=False)]
  transfers between devices with their start and end apart: 6 -> 5, of which waited for: 6 -> 5; matrix products, arithmetic and copies ran while one was open for 3% -> 2% of each run, Pallas kernels for 0% -> 0%
where the time goes in v7:
time: 163 us
  blocking collectives  65.4 us (40%)
  waiting for transfers between devices  43.1 us (26%)
  starting transfers between devices  34.4 us (21%)
  local copies, waits for them, and re-layouts  10.2 us (6%)
  other arithmetic  4.13 us (3%)
  matrix products  4.08 us (3%)
    all_to_all x3, blocking collectives, gather_all(): return lax.all_to_all(spread, axis, 0, 0, tiled=False)  41.2 us
    all_to_all x3, waiting for transfers between devices, gather_all(): return lax.all_to_all(spread, axis, 0, 0, tiled=False)  22.6 us
    all_to_all x2, waiting for transfers between devices, reduce_rows(): packed = jnp.sum(lax.all_to_all(split, axis, 0, 0, tiled=False), axis=0)  20.5 us
    all_to_all x3, starting transfers between devices, gather_all(): return lax.all_to_all(spread, axis, 0, 0, tiled=False)  19.8 us
    all_to_all x1, blocking collectives, per_device(): lax.all_to_all(sent, 'pz', 0, 0, tiled=False)  14.8 us
    all_to_all x2, starting transfers between devices, reduce_rows(): packed = jnp.sum(lax.all_to_all(split, axis, 0, 0, tiled=False), axis=0)  14.6 us
    all_to_all x1, blocking collectives, per_device(): stage = merge_blocks(lax.all_to_all(sent, 'px', 0, 0, tiled=False), share)  9.33 us
  transfers between devices with their start and end apart: 5, of which 5 were waited for; matrix products, arithmetic and copies ran while one was open for 2% of the time, Pallas kernels for 0%

profile of v7, /device:TPU:1, one launch (start us, length us, event | category | flops | bytes accessed | tf_op | source)
XLA Modules:
  0.0 162.5 jit_solution(2424737051820969083)
XLA Ops:
  0.7 0.8 broadcast_subtract_fusion
  1.5 0.3 copy-done
  1.8 0.6 fusion.5
  2.4 0.7 broadcast_in_dim.201
  3.2 10.1 %all-to-all-start = ((bf16[8,128,112]{1,2,0:T(8,128)(2,1)}), bf16[8,128,112]{1,2,0:T(8,128)(2,1)S(1)}, u32[]{:S(2)}, u32[]{:S(2)}) async-start(bf16[8,128,112]{1,2,0:T(8,128)(2,1)} %broadcast_in_dim.201), calls=%async_computation | async-start | bytes 458752 | tf_op jit(solution)/shard_map/all_to_all | solution.py:62
  13.3 0.2 fusion.37
  13.5 0.2 compare_reduce_fusion
  13.8 5.7 %all-to-all-done = bf16[8,128,112]{1,2,0:T(8,128)(2,1)S(1)} async-done(((bf16[8,128,112]{1,2,0:T(8,128)(2,1)}), bf16[8,128,112]{1,2,0:T(8,128)(2,1)S(1)}, u32[]{:S(2)}, u32[]{:S(2)}) %all-to-all-start) | async-done | bytes 229408 | tf_op jit(solution)/shard_map/all_to_all | solution.py:62
  19.6 0.2 concatenate.36
  19.8 0.3 fusion.48
  20.1 0.9 concatenate.30
  21.0 3.6 %all-to-all-start.1 = ((f32[4,32,1280]{2,1,0:T(8,128)}), f32[4,32,1280]{2,1,0:T(8,128)S(1)}, u32[]{:S(2)}, u32[]{:S(2)}) async-start(f32[4,32,1280]{2,1,0:T(8,128)} %concatenate.30), calls=%async_computation.1 | async-start | bytes 1310720 | tf_op jit(solution)/shard_map/all_to_all | solution.py:76
  24.7 0.6 gather_fusion.1
  25.3 0.6 gather_fusion
  26.0 8.6 %all-to-all-done.1 = f32[4,32,1280]{2,1,0:T(8,128)S(1)} async-done(((f32[4,32,1280]{2,1,0:T(8,128)}), f32[4,32,1280]{2,1,0:T(8,128)S(1)}, u32[]{:S(2)}, u32[]{:S(2)}) %all-to-all-start.1) | async-done | bytes 655392 | tf_op jit(solution)/shard_map/all_to_all | solution.py:76
  34.7 0.8 reshape.639
  35.4 11.0 %all-to-all-start.2 = ((f32[16,2,1280]{2,1,0:T(2,128)}), f32[16,2,1280]{2,1,0:T(2,128)S(1)}, u32[]{:S(2)}, u32[]{:S(2)}) async-start(f32[16,2,1280]{2,1,0:T(2,128)} %reshape.639), calls=%async_computation.2 | async-start | bytes 327680 | tf_op jit(solution)/shard_map/all_to_all | solution.py:76
  46.6 11.9 %all-to-all-done.2 = f32[16,2,1280]{2,1,0:T(2,128)S(1)} async-done(((f32[16,2,1280]{2,1,0:T(2,128)}), f32[16,2,1280]{2,1,0:T(2,128)S(1)}, u32[]{:S(2)}, u32[]{:S(2)}) %all-to-all-start.2) | async-done | bytes 163872 | tf_op jit(solution)/shard_map/all_to_all | solution.py:76
  59.0 0.7 broadcast_in_dim.203
  59.7 6.2 %all-to-all-start.3 = ((bf16[16,2,1152]{2,1,0:T(2,128)(2,1)}), bf16[16,2,1152]{2,1,0:T(2,128)(2,1)S(1)}, u32[]{:S(2)}, u32[]{:S(2)}) async-start(bf16[16,2,1152]{2,1,0:T(2,128)(2,1)} %broadcast_in_dim.203), calls=%async_computation.3 | async-start | bytes 147456 | tf_op jit(solution)/shard_map/all_to_all | solution.py:62
  66.0 0.3 fusion.3
  66.4 11.3 %all-to-all-done.3 = bf16[16,2,1152]{2,1,0:T(2,128)(2,1)S(1)} async-done(((bf16[16,2,1152]{2,1,0:T(2,128)(2,1)}), bf16[16,2,1152]{2,1,0:T(2,128)(2,1)S(1)}, u32[]{:S(2)}, u32[]{:S(2)}) %all-to-all-start.3) | async-done | bytes 73760 | tf_op jit(solution)/shard_map/all_to_all | solution.py:62
  77.7 0.7 broadcast_in_dim.205
  78.4 3.5 %all-to-all-start.4 = ((bf16[4,32,1152]{2,1,0:T(8,128)(2,1)}), bf16[4,32,1152]{2,1,0:T(8,128)(2,1)S(1)}, u32[]{:S(2)}, u32[]{:S(2)}) async-start(bf16[4,32,1152]{2,1,0:T(8,128)(2,1)} %broadcast_in_dim.205), calls=%async_computation.4 | async-start | bytes 589824 | tf_op jit(solution)/shard_map/all_to_all | solution.py:62
  81.9 5.6 %all-to-all-done.4 = bf16[4,32,1152]{2,1,0:T(8,128)(2,1)S(1)} async-done(((bf16[4,32,1152]{2,1,0:T(8,128)(2,1)}), bf16[4,32,1152]{2,1,0:T(8,128)(2,1)S(1)}, u32[]{:S(2)}, u32[]{:S(2)}) %all-to-all-start.4) | async-done | bytes 294944 | tf_op jit(solution)/shard_map/all_to_all | solution.py:62
  87.5 0.2 reshape_reshape.6
  87.9 0.6 gather_fusion.2
  88.7 0.2 copy-done.6
  88.9 0.4 fusion.71
  89.4 0.6 gather_fusion.3
  90.0 0.4 fusion.18
  90.5 0.3 convolution_multiply_fusion.1
  91.2 0.3 fusion.2
  91.6 0.7 copy-done.2
  92.3 0.5 fusion.72
  92.9 0.4 fusion.16
  93.5 0.4 fusion.14
  94.1 0.5 fusion.8
  94.7 0.3 add_select_fusion
  95.1 9.3 %all_to_all.50 = f32[4,16,16,128]{3,2,1,0:T(8,128)S(1)} all-to-all(f32[4,16,16,128]{3,2,1,0:T(8,128)S(1)} %pad_maximum_fusion), channel_id=1, replica_groups=mesh['kv'=8,'px'=4,'pz'=16] {'px'}, dimensions={0} | all-to-all | bytes 1048576 | tf_op jit(solution)/shard_map/all_to_all | solution.py:251
  104.6 0.2 fusion.7
  104.8 14.8 %all_to_all.51 = f32[16,16,128]{2,1,0:T(8,128)S(1)} all-to-all(f32[16,16,128]{2,1,0:T(8,128)S(1)} %pad_maximum_fusion.2), channel_id=1, replica_groups=mesh['kv'=8,'px'=4,'pz'=16] {'pz'}, dimensions={0} | all-to-all | bytes 262144 | tf_op jit(solution)/shard_map/all_to_all | solution.py:253
  119.9 15.5 %all_to_all.52 = bf16[16,14,128]{2,1,0:T(8,128)(2,1)S(1)} all-to-all(bf16[16,14,128]{2,1,0:T(8,128)(2,1)S(1)} %broadcast_in_dim.219), channel_id=1, replica_groups=mesh['kv'=8,'px'=4,'pz'=16] {'pz'}, dimensions={0} | all-to-all | bytes 114688 | tf_op jit(solution)/shard_map/all_to_all | solution.py:62
  135.5 7.8 %all_to_all.53 = bf16[4,224,128]{2,1,0:T(8,128)(2,1)S(1)} all-to-all(bf16[4,224,128]{2,1,0:T(8,128)(2,1)S(1)} %broadcast_in_dim.221), channel_id=1, replica_groups=mesh['kv'=8,'px'=4,'pz'=16] {'px'}, dimensions={0} | all-to-all | bytes 458752 | tf_op jit(solution)/shard_map/all_to_all | solution.py:62
  143.3 0.2 reshape_reshape.7
  143.6 0.2 convolution_convert_fusion.2
  143.8 17.9 %all_to_all.54 = bf16[8,128,112]{1,2,0:T(8,128)(2,1)S(1)} all-to-all(bf16[8,128,112]{1,2,0:T(8,128)(2,1)S(1)} %broadcast_in_dim.222), channel_id=1, replica_groups=mesh['kv'=8,'px'=4,'pz'=16] {'kv'}, dimensions={0} | all-to-all | bytes 458752 | tf_op jit(solution)/shard_map/all_to_all | solution.py:62
  161.8 0.7 copy.252
  (94 shorter events, 3.2 us)
Async XLA Ops:
  0.6 1.2 copy-start
  1.8 11.5 %copy-start.7 = (s32[8,64]{1,0:T(8,128)S(1)}, s32[8,64]{1,0:T(8,128)}, u32[]{:S(2)}) copy-start(s32[8,64]{1,0:T(8,128)} %param.12) | copy-start | bytes 6148
  1.8 11.9 %copy-start.9 = (bf16[112]{0:T(256)(128)(2,1)S(1)}, bf16[112]{0:T(256)(128)(2,1)}, u32[]{:S(2)}) copy-start(bf16[112]{0:T(256)(128)(2,1)} %param.15) | copy-start | bytes 676
  2.4 17.3 %copy-start.4 = (bf16[112,1152]{1,0:T(8,128)(2,1)S(1)}, bf16[112,1152]{1,0:T(8,128)(2,1)}, u32[]{:S(2)}) copy-start(bf16[112,1152]{1,0:T(8,128)(2,1)} %param.16) | copy-start | bytes 774148
  3.2 16.3 %all-to-all-start = ((bf16[8,128,112]{1,2,0:T(8,128)(2,1)}), bf16[8,128,112]{1,2,0:T(8,128)(2,1)S(1)}, u32[]{:S(2)}, u32[]{:S(2)}) async-start(bf16[8,128,112]{1,2,0:T(8,128)(2,1)} %broadcast_in_dim.201), calls=%async_computation | async-start | bytes 458752 | tf_op jit(solution)/shard_map/all_to_all | solution.py:62
  21.0 3.6 %copy-start.1 = (s32[8]{0:T(128)S(1)}, s32[8]{0:T(128)}, u32[]{:S(2)}) copy-start(s32[8]{0:T(128)} %param.11) | copy-start | bytes 100
  21.0 4.9 %copy-start.8 = (s32[2,64]{1,0:T(2,128)S(1)}, s32[2,64]{1,0:T(2,128)}, u32[]{:S(2)}) copy-start(s32[2,64]{1,0:T(2,128)} %param.13) | copy-start | bytes 1540
  21.0 13.6 %all-to-all-start.1 = ((f32[4,32,1280]{2,1,0:T(8,128)}), f32[4,32,1280]{2,1,0:T(8,128)S(1)}, u32[]{:S(2)}, u32[]{:S(2)}) async-start(f32[4,32,1280]{2,1,0:T(8,128)} %concatenate.30), calls=%async_computation.1 | async-start | bytes 1310720 | tf_op jit(solution)/shard_map/all_to_all | solution.py:76
  26.0 40.0 %copy-start.3 = (bf16[2,64,13,128]{3,1,2,0:T(8,128)(2,1)S(1)}, bf16[2,64,13,128]{3,1,2,0:T(8,128)(2,1)}, u32[]{:S(2)}) copy-start(bf16[2,64,13,128]{3,1,2,0:T(8,128)(2,1)} %param.18) | copy-start | bytes 1277956
  35.4 23.1 %all-to-all-start.2 = ((f32[16,2,1280]{2,1,0:T(2,128)}), f32[16,2,1280]{2,1,0:T(2,128)S(1)}, u32[]{:S(2)}, u32[]{:S(2)}) async-start(f32[16,2,1280]{2,1,0:T(2,128)} %reshape.639), calls=%async_computation.2 | async-start | bytes 327680 | tf_op jit(solution)/shard_map/all_to_all | solution.py:76
  59.7 17.9 %all-to-all-start.3 = ((bf16[16,2,1152]{2,1,0:T(2,128)(2,1)}), bf16[16,2,1152]{2,1,0:T(2,128)(2,1)S(1)}, u32[]{:S(2)}, u32[]{:S(2)}) async-start(bf16[16,2,1152]{2,1,0:T(2,128)(2,1)} %broadcast_in_dim.203), calls=%async_computation.3 | async-start | bytes 147456 | tf_op jit(solution)/shard_map/all_to_all | solution.py:62
  78.4 9.1 %all-to-all-start.4 = ((bf16[4,32,1152]{2,1,0:T(8,128)(2,1)}), bf16[4,32,1152]{2,1,0:T(8,128)(2,1)S(1)}, u32[]{:S(2)}, u32[]{:S(2)}) async-start(bf16[4,32,1152]{2,1,0:T(8,128)(2,1)} %broadcast_in_dim.205), calls=%async_computation.4 | async-start | bytes 589824 | tf_op jit(solution)/shard_map/all_to_all | solution.py:62
  87.9 1.0 copy-start.6
  91.5 0.8 copy-start.2
  119.6 23.9 %copy-start.5 = (bf16[896,112]{0,1:T(8,128)(2,1)S(1)}, bf16[896,112]{0,1:T(8,128)(2,1)}, u32[]{:S(2)}) copy-start(bf16[896,112]{0,1:T(8,128)(2,1)} %param.17) | copy-start | bytes 602116

commit v8 on v7

--- a/solution.py
+++ b/solution.py
@@ -186,7 +186,13 @@
     )
     live_full = live_tok[None, :, None, :]
     grouped = queries.reshape(num_steps, GROUPS, BEAMS, local_heads, PER_KV, HEAD_DIM)
-    chosen = jnp.take(grouped, owner_group, axis=1)
+    owner = owner_group[:, None] == jnp.arange(GROUPS, dtype=jnp.int32)[None, :]
+    chosen = jnp.einsum(
+        "sg,tgbkhd->tsbkhd",
+        owner.astype(jnp.bfloat16),
+        grouped,
+        preferred_element_type=jnp.float32,
+    ).astype(jnp.bfloat16)
     query_rows = num_steps * BEAMS * PER_KV
     chosen = jnp.transpose(chosen, (3, 1, 0, 2, 4, 5)).reshape(
         local_heads, slot_rows, query_rows, HEAD_DIM
@@ -216,7 +222,9 @@
     ]
     spread = jnp.where(member[None, :, :, None], slot_peak[:, :, None, :], NEGATIVE)
     group_peak = jnp.max(spread, axis=1)
-    slot_base = jnp.take(group_peak, owner_group, axis=1)
+    slot_base = jnp.max(
+        jnp.where(owner[None, :, :, None], group_peak[:, None, :, :], -jnp.inf), axis=2
+    )
     weight = jnp.where(slot_used[None, :, None], jnp.exp(slot_peak - slot_base), 0.0)
     member_f = member.astype(jnp.float32)
     group_total = jnp.einsum(
@@ -251,8 +259,12 @@
     stage = merge_blocks(lax.all_to_all(sent, "px", 0, 0, tiled=False), share)
     sent = pack_blocks(*stage, share)
     top, total, acc = merge_blocks(lax.all_to_all(sent, "pz", 0, 0, tiled=False), share)
-    attended_mine = (acc / total[:, None]).astype(jnp.bfloat16)
-    attended = gather_rows(attended_mine)
+    inner_spread = (inner_count, *acc.shape)
+    attended_mine = (
+        jnp.broadcast_to(acc[None], inner_spread) / jnp.broadcast_to(total[None, :, None], inner_spread)
+    ).astype(jnp.bfloat16)
+    attended = lax.all_to_all(attended_mine, "pz", 0, 0, tiled=False).reshape(-1, HEAD_DIM)
+    attended = gather_all(attended, "px").reshape(-1, HEAD_DIM)
     flat_heads = attended.reshape(row_count, local_heads * PER_KV * HEAD_DIM)
     head_terms = jnp.dot(flat_heads, w_out, preferred_element_type=jnp.float32)
     shared = gather_all(head_terms.astype(jnp.bfloat16), "kv").astype(jnp.float32)

time: 163 us -> 164 us (level)
  matrix products: 4.08 us -> 6.27 us
    all_to_all x0 -> x1, blocking collectives: none -> 15.5 us  [per_device(): lax.all_to_all(attended_mine, 'pz', 0, 0, tiled=False).reshape(-1, HEAD_DIM)]
    all_to_all x3 -> x2, blocking collectives: 41.2 us -> 25.7 us  [gather_all(): return lax.all_to_all(spread, axis, 0, 0, tiled=False)]
where the time goes in v8:
time: 164 us; the launch traced here: 163 us
  blocking collectives  65.4 us (40%)
  waiting for transfers between devices  43 us (26%)
  starting transfers between devices  34.4 us (21%)
  local copies, waits for them, and re-layouts  8.8 us (5%)
  matrix products  6.27 us (4%)
  other arithmetic  4.14 us (3%)
    all_to_all x2, blocking collectives, gather_all(): return lax.all_to_all(spread, axis, 0, 0, tiled=False)  25.7 us
    all_to_all x3, waiting for transfers between devices, gather_all(): return lax.all_to_all(spread, axis, 0, 0, tiled=False)  22.5 us
    all_to_all x2, waiting for transfers between devices, reduce_rows(): packed = jnp.sum(lax.all_to_all(split, axis, 0, 0, tiled=False), axis=0)  20.5 us
    all_to_all x3, starting transfers between devices, gather_all(): return lax.all_to_all(spread, axis, 0, 0, tiled=False)  19.8 us
    all_to_all x1, blocking collectives, per_device(): lax.all_to_all(attended_mine, 'pz', 0, 0, tiled=False).reshape(-1, HEAD_DIM)  15.5 us
    all_to_all x1, blocking collectives, per_device(): lax.all_to_all(sent, 'pz', 0, 0, tiled=False)  14.8 us
    all_to_all x2, starting transfers between devices, reduce_rows(): packed = jnp.sum(lax.all_to_all(split, axis, 0, 0, tiled=False), axis=0)  14.6 us
    all_to_all x1, blocking collectives, per_device(): stage = merge_blocks(lax.all_to_all(sent, 'px', 0, 0, tiled=False), share)  9.33 us
  transfers between devices with their start and end apart: 5, of which 5 were waited for; matrix products, arithmetic and copies ran while one was open for 2% of the time, Pallas kernels for 0%

profile of v8, /device:TPU:1, one launch (start us, length us, event | category | flops | bytes accessed | tf_op | source)
XLA Modules:
  0.0 163.2 jit_solution(1241299156351868585)
XLA Ops:
  0.7 0.8 broadcast_subtract_fusion
  1.5 0.3 copy-done
  1.8 0.6 fusion.5
  2.4 0.7 broadcast_in_dim.140
  3.2 10.1 %all-to-all-start = ((bf16[8,128,112]{1,2,0:T(8,128)(2,1)}), bf16[8,128,112]{1,2,0:T(8,128)(2,1)S(1)}, u32[]{:S(2)}, u32[]{:S(2)}) async-start(bf16[8,128,112]{1,2,0:T(8,128)(2,1)} %broadcast_in_dim.140), calls=%async_computation | async-start | bytes 458752 | tf_op jit(solution)/shard_map/all_to_all | solution.py:62
  13.3 0.2 fusion.37
  13.5 0.2 compare_reduce_fusion
  13.8 5.7 %all-to-all-done = bf16[8,128,112]{1,2,0:T(8,128)(2,1)S(1)} async-done(((bf16[8,128,112]{1,2,0:T(8,128)(2,1)}), bf16[8,128,112]{1,2,0:T(8,128)(2,1)S(1)}, u32[]{:S(2)}, u32[]{:S(2)}) %all-to-all-start) | async-done | bytes 229408 | tf_op jit(solution)/shard_map/all_to_all | solution.py:62
  19.6 0.2 concatenate.36
  19.8 0.3 fusion.48
  20.1 0.9 concatenate.30
  21.0 3.6 %all-to-all-start.1 = ((f32[4,32,1280]{2,1,0:T(8,128)}), f32[4,32,1280]{2,1,0:T(8,128)S(1)}, u32[]{:S(2)}, u32[]{:S(2)}) async-start(f32[4,32,1280]{2,1,0:T(8,128)} %concatenate.30), calls=%async_computation.1 | async-start | bytes 1310720 | tf_op jit(solution)/shard_map/all_to_all | solution.py:76
  24.7 0.6 gather_fusion.1
  25.3 0.6 gather_fusion
  26.1 8.6 %all-to-all-done.1 = f32[4,32,1280]{2,1,0:T(8,128)S(1)} async-done(((f32[4,32,1280]{2,1,0:T(8,128)}), f32[4,32,1280]{2,1,0:T(8,128)S(1)}, u32[]{:S(2)}, u32[]{:S(2)}) %all-to-all-start.1) | async-done | bytes 655392 | tf_op jit(solution)/shard_map/all_to_all | solution.py:76
  34.6 0.8 reshape.630
  35.4 11.0 %all-to-all-start.2 = ((f32[16,2,1280]{2,1,0:T(2,128)}), f32[16,2,1280]{2,1,0:T(2,128)S(1)}, u32[]{:S(2)}, u32[]{:S(2)}) async-start(f32[16,2,1280]{2,1,0:T(2,128)} %reshape.630), calls=%async_computation.2 | async-start | bytes 327680 | tf_op jit(solution)/shard_map/all_to_all | solution.py:76
  46.6 12.0 %all-to-all-done.2 = f32[16,2,1280]{2,1,0:T(2,128)S(1)} async-done(((f32[16,2,1280]{2,1,0:T(2,128)}), f32[16,2,1280]{2,1,0:T(2,128)S(1)}, u32[]{:S(2)}, u32[]{:S(2)}) %all-to-all-start.2) | async-done | bytes 163872 | tf_op jit(solution)/shard_map/all_to_all | solution.py:76
  58.6 0.1 fusion.60
  59.0 0.7 broadcast_in_dim.211
  59.7 6.2 %all-to-all-start.3 = ((bf16[16,2,1152]{2,1,0:T(2,128)(2,1)}), bf16[16,2,1152]{2,1,0:T(2,128)(2,1)S(1)}, u32[]{:S(2)}, u32[]{:S(2)}) async-start(bf16[16,2,1152]{2,1,0:T(2,128)(2,1)} %broadcast_in_dim.211), calls=%async_computation.3 | async-start | bytes 147456 | tf_op jit(solution)/shard_map/all_to_all | solution.py:62
  66.1 0.3 fusion.3
  66.4 11.2 %all-to-all-done.3 = bf16[16,2,1152]{2,1,0:T(2,128)(2,1)S(1)} async-done(((bf16[16,2,1152]{2,1,0:T(2,128)(2,1)}), bf16[16,2,1152]{2,1,0:T(2,128)(2,1)S(1)}, u32[]{:S(2)}, u32[]{:S(2)}) %all-to-all-start.3) | async-done | bytes 73760 | tf_op jit(solution)/shard_map/all_to_all | solution.py:62
  77.6 0.7 broadcast_in_dim.213
  78.4 3.5 %all-to-all-start.4 = ((bf16[4,32,1152]{2,1,0:T(8,128)(2,1)}), bf16[4,32,1152]{2,1,0:T(8,128)(2,1)S(1)}, u32[]{:S(2)}, u32[]{:S(2)}) async-start(bf16[4,32,1152]{2,1,0:T(8,128)(2,1)} %broadcast_in_dim.213), calls=%async_computation.4 | async-start | bytes 589824 | tf_op jit(solution)/shard_map/all_to_all | solution.py:62
  81.9 5.6 %all-to-all-done.4 = bf16[4,32,1152]{2,1,0:T(8,128)(2,1)S(1)} async-done(((bf16[4,32,1152]{2,1,0:T(8,128)(2,1)}), bf16[4,32,1152]{2,1,0:T(8,128)(2,1)S(1)}, u32[]{:S(2)}, u32[]{:S(2)}) %all-to-all-start.4) | async-done | bytes 294944 | tf_op jit(solution)/shard_map/all_to_all | solution.py:62
  87.5 0.2 reshape_reshape.6
  87.8 0.3 convolution_convert_fusion.2
  88.1 1.3 fusion.73
  89.4 0.4 fusion.18
  90.2 1.3 convolution_multiply_fusion.1
  91.5 0.1 convolution_bitcast_fusion
  91.8 0.3 fusion.2
  92.3 0.7 copy-done.2
  93.0 0.5 fusion.74
  93.6 0.4 fusion.16
  94.2 0.4 fusion.14
  94.8 0.5 fusion.8
  95.3 0.3 add_select_fusion
  95.8 9.3 %all_to_all.50 = f32[4,16,16,128]{3,2,1,0:T(8,128)S(1)} all-to-all(f32[4,16,16,128]{3,2,1,0:T(8,128)S(1)} %pad_maximum_fusion), channel_id=1, replica_groups=mesh['kv'=8,'px'=4,'pz'=16] {'px'}, dimensions={0} | all-to-all | bytes 1048576 | tf_op jit(solution)/shard_map/all_to_all | solution.py:259
  105.2 0.2 fusion.7
  105.5 14.8 %all_to_all.51 = f32[16,16,128]{2,1,0:T(8,128)S(1)} all-to-all(f32[16,16,128]{2,1,0:T(8,128)S(1)} %pad_maximum_fusion.2), channel_id=1, replica_groups=mesh['kv'=8,'px'=4,'pz'=16] {'pz'}, dimensions={0} | all-to-all | bytes 262144 | tf_op jit(solution)/shard_map/all_to_all | solution.py:261
  120.6 15.5 %all_to_all.52 = bf16[16,14,128]{2,1,0:T(8,128)(2,1)S(1)} all-to-all(bf16[16,14,128]{2,1,0:T(8,128)(2,1)S(1)} %divide_convert_fusion), channel_id=1, replica_groups=mesh['kv'=8,'px'=4,'pz'=16] {'pz'}, dimensions={0} | all-to-all | bytes 114688 | tf_op jit(solution)/shard_map/all_to_all | solution.py:266
  136.2 7.8 %all_to_all.53 = bf16[4,224,128]{2,1,0:T(8,128)(2,1)S(1)} all-to-all(bf16[4,224,128]{2,1,0:T(8,128)(2,1)S(1)} %broadcast_in_dim.230), channel_id=1, replica_groups=mesh['kv'=8,'px'=4,'pz'=16] {'px'}, dimensions={0} | all-to-all | bytes 458752 | tf_op jit(solution)/shard_map/all_to_all | solution.py:62
  144.0 0.2 reshape_reshape.7
  144.3 0.2 convolution_convert_fusion.3
  144.5 17.9 %all_to_all.54 = bf16[8,128,112]{1,2,0:T(8,128)(2,1)S(1)} all-to-all(bf16[8,128,112]{1,2,0:T(8,128)(2,1)S(1)} %broadcast_in_dim.231), channel_id=1, replica_groups=mesh['kv'=8,'px'=4,'pz'=16] {'kv'}, dimensions={0} | all-to-all | bytes 458752 | tf_op jit(solution)/shard_map/all_to_all | solution.py:62
  162.5 0.7 copy.266
  (89 shorter events, 3.0 us)
Async XLA Ops:
  0.6 1.2 copy-start
  1.8 11.5 %copy-start.6 = (s32[8,64]{1,0:T(8,128)S(1)}, s32[8,64]{1,0:T(8,128)}, u32[]{:S(2)}) copy-start(s32[8,64]{1,0:T(8,128)} %param.12) | copy-start | bytes 6148
  1.8 11.9 %copy-start.8 = (bf16[112]{0:T(256)(128)(2,1)S(1)}, bf16[112]{0:T(256)(128)(2,1)}, u32[]{:S(2)}) copy-start(bf16[112]{0:T(256)(128)(2,1)} %param.15) | copy-start | bytes 676
  1.8 11.9 %copy-start.7 = (s32[2,64]{1,0:T(2,128)S(1)}, s32[2,64]{1,0:T(2,128)}, u32[]{:S(2)}) copy-start(s32[2,64]{1,0:T(2,128)} %param.13) | copy-start | bytes 1540
  2.4 17.3 %copy-start.4 = (bf16[112,1152]{1,0:T(8,128)(2,1)S(1)}, bf16[112,1152]{1,0:T(8,128)(2,1)}, u32[]{:S(2)}) copy-start(bf16[112,1152]{1,0:T(8,128)(2,1)} %param.16) | copy-start | bytes 774148
  3.2 16.3 %all-to-all-start = ((bf16[8,128,112]{1,2,0:T(8,128)(2,1)}), bf16[8,128,112]{1,2,0:T(8,128)(2,1)S(1)}, u32[]{:S(2)}, u32[]{:S(2)}) async-start(bf16[8,128,112]{1,2,0:T(8,128)(2,1)} %broadcast_in_dim.140), calls=%async_computation | async-start | bytes 458752 | tf_op jit(solution)/shard_map/all_to_all | solution.py:62
  21.0 3.6 %copy-start.1 = (s32[8]{0:T(128)S(1)}, s32[8]{0:T(128)}, u32[]{:S(2)}) copy-start(s32[8]{0:T(128)} %param.11) | copy-start | bytes 100
  21.0 13.6 %all-to-all-start.1 = ((f32[4,32,1280]{2,1,0:T(8,128)}), f32[4,32,1280]{2,1,0:T(8,128)S(1)}, u32[]{:S(2)}, u32[]{:S(2)}) async-start(f32[4,32,1280]{2,1,0:T(8,128)} %concatenate.30), calls=%async_computation.1 | async-start | bytes 1310720 | tf_op jit(solution)/shard_map/all_to_all | solution.py:76
  26.0 40.0 %copy-start.3 = (bf16[2,64,13,128]{3,1,2,0:T(8,128)(2,1)S(1)}, bf16[2,64,13,128]{3,1,2,0:T(8,128)(2,1)}, u32[]{:S(2)}) copy-start(bf16[2,64,13,128]{3,1,2,0:T(8,128)(2,1)} %param.18) | copy-start | bytes 1277956
  35.4 23.1 %all-to-all-start.2 = ((f32[16,2,1280]{2,1,0:T(2,128)}), f32[16,2,1280]{2,1,0:T(2,128)S(1)}, u32[]{:S(2)}, u32[]{:S(2)}) async-start(f32[16,2,1280]{2,1,0:T(2,128)} %reshape.630), calls=%async_computation.2 | async-start | bytes 327680 | tf_op jit(solution)/shard_map/all_to_all | solution.py:76
  59.7 17.9 %all-to-all-start.3 = ((bf16[16,2,1152]{2,1,0:T(2,128)(2,1)}), bf16[16,2,1152]{2,1,0:T(2,128)(2,1)S(1)}, u32[]{:S(2)}, u32[]{:S(2)}) async-start(bf16[16,2,1152]{2,1,0:T(2,128)(2,1)} %broadcast_in_dim.211), calls=%async_computation.3 | async-start | bytes 147456 | tf_op jit(solution)/shard_map/all_to_all | solution.py:62
  78.4 9.1 %all-to-all-start.4 = ((bf16[4,32,1152]{2,1,0:T(8,128)(2,1)}), bf16[4,32,1152]{2,1,0:T(8,128)(2,1)S(1)}, u32[]{:S(2)}, u32[]{:S(2)}) async-start(bf16[4,32,1152]{2,1,0:T(8,128)(2,1)} %broadcast_in_dim.213), calls=%async_computation.4 | async-start | bytes 589824 | tf_op jit(solution)/shard_map/all_to_all | solution.py:62
  92.2 0.8 copy-start.2
  120.3 23.9 %copy-start.5 = (bf16[896,112]{0,1:T(8,128)(2,1)S(1)}, bf16[896,112]{0,1:T(8,128)(2,1)}, u32[]{:S(2)}) copy-start(bf16[896,112]{0,1:T(8,128)(2,1)} %param.17) | copy-start | bytes 602116

commit v9 on v7

--- a/solution.py
+++ b/solution.py
@@ -63,7 +63,8 @@
 
 
 def gather_rows(part):
-    inner = gather_all(part, "pz")
+    lanes = part.reshape(-1, HEAD_DIM)
+    inner = gather_all(lanes, "pz")
     inner = inner.reshape(-1, *part.shape[1:])
     outer = gather_all(inner, "px")
     return outer.reshape(-1, *part.shape[1:])
@@ -72,8 +73,9 @@
 def reduce_rows(packed):
     for axis in ("px", "pz"):
         sources = lax.axis_size(axis)
-        split = packed.reshape(sources, packed.shape[0] // sources, *packed.shape[1:])
-        packed = jnp.sum(lax.all_to_all(split, axis, 0, 0, tiled=False), axis=0)
+        block = (packed.shape[0] // sources, *packed.shape[1:])
+        split = packed.reshape(sources, -1, HEAD_DIM)
+        packed = jnp.sum(lax.all_to_all(split, axis, 0, 0, tiled=False), axis=0).reshape(block)
     return packed
 
 

time: 163 us -> 165 us (1.012)
  transfers between devices with their start and end apart: 5 -> 5, of which waited for: 5 -> 5; matrix products, arithmetic and copies ran while one was open for 2% -> 1% of each run, Pallas kernels for 0% -> 0%
where the time goes in v9:
time: 165 us; the launch traced here: 164 us
  blocking collectives  66 us (40%)
  waiting for transfers between devices  43.4 us (26%)
  starting transfers between devices  35.4 us (21%)
  local copies, waits for them, and re-layouts  10.2 us (6%)
  matrix products  4.09 us (2%)
  other arithmetic  4.07 us (2%)
    all_to_all x3, blocking collectives, gather_all(): return lax.all_to_all(spread, axis, 0, 0, tiled=False)  41.4 us
    all_to_all x3, waiting for transfers between devices, gather_all(): return lax.all_to_all(spread, axis, 0, 0, tiled=False)  22.7 us
    all_to_all x3, starting transfers between devices, gather_all(): return lax.all_to_all(spread, axis, 0, 0, tiled=False)  20.8 us
    all_to_all x2, waiting for transfers between devices, reduce_rows(): lax.all_to_all(split, axis, 0, 0, tiled=False)  20.7 us
    all_to_all x1, blocking collectives, per_device(): lax.all_to_all(sent, 'pz', 0, 0, tiled=False)  15.3 us
    all_to_all x2, starting transfers between devices, reduce_rows(): lax.all_to_all(split, axis, 0, 0, tiled=False)  14.6 us
    all_to_all x1, blocking collectives, per_device(): stage = merge_blocks(lax.all_to_all(sent, 'px', 0, 0, tiled=False), share)  9.33 us
  transfers between devices with their start and end apart: 5, of which 5 were waited for; matrix products, arithmetic and copies ran while one was open for 1% of the time, Pallas kernels for 0%

profile of v9, /device:TPU:1, one launch (start us, length us, event | category | flops | bytes accessed | tf_op | source)
XLA Modules:
  0.0 164.4 jit_solution(11649612611370186276)
XLA Ops:
  0.7 0.8 broadcast_subtract_fusion
  1.5 0.3 copy-done
  1.8 0.6 fusion.5
  2.4 0.7 broadcast_in_dim.203
  3.2 10.1 %all-to-all-start = ((bf16[8,128,112]{1,2,0:T(8,128)(2,1)}), bf16[8,128,112]{1,2,0:T(8,128)(2,1)S(1)}, u32[]{:S(2)}, u32[]{:S(2)}) async-start(bf16[8,128,112]{1,2,0:T(8,128)(2,1)} %broadcast_in_dim.203), calls=%async_computation | async-start | bytes 458752 | tf_op jit(solution)/shard_map/all_to_all | solution.py:62
  13.3 0.2 fusion.37
  13.5 0.2 compare_reduce_fusion
  13.8 5.7 %all-to-all-done = bf16[8,128,112]{1,2,0:T(8,128)(2,1)S(1)} async-done(((bf16[8,128,112]{1,2,0:T(8,128)(2,1)}), bf16[8,128,112]{1,2,0:T(8,128)(2,1)S(1)}, u32[]{:S(2)}, u32[]{:S(2)}) %all-to-all-start) | async-done | bytes 229408 | tf_op jit(solution)/shard_map/all_to_all | solution.py:62
  19.7 0.3 fusion.48
  20.1 0.9 reshape.637
  21.0 3.6 %all-to-all-start.1 = ((f32[4,320,128]{2,1,0:T(8,128)}), f32[4,320,128]{2,1,0:T(8,128)S(1)}, u32[]{:S(2)}, u32[]{:S(2)}) async-start(f32[4,320,128]{2,1,0:T(8,128)} %reshape.637), calls=%async_computation.1 | async-start | bytes 1310720 | tf_op jit(solution)/shard_map/all_to_all | solution.py:78
  24.6 0.6 gather_fusion.1
  25.3 0.6 gather_fusion
  26.0 8.6 %all-to-all-done.1 = f32[4,320,128]{2,1,0:T(8,128)S(1)} async-done(((f32[4,320,128]{2,1,0:T(8,128)}), f32[4,320,128]{2,1,0:T(8,128)S(1)}, u32[]{:S(2)}, u32[]{:S(2)}) %all-to-all-start.1) | async-done | bytes 655392 | tf_op jit(solution)/shard_map/all_to_all | solution.py:78
  34.6 0.7 reshape_reshape.9
  35.3 11.0 %all-to-all-start.2 = ((f32[16,20,128]{2,1,0:T(8,128)}), f32[16,20,128]{2,1,0:T(8,128)S(1)}, u32[]{:S(2)}, u32[]{:S(2)}) async-start(f32[16,20,128]{2,1,0:T(8,128)} %reshape_reshape.9), calls=%async_computation.2 | async-start | bytes 393216 | tf_op jit(solution)/shard_map/all_to_all | solution.py:78
  46.5 12.1 %all-to-all-done.2 = f32[16,20,128]{2,1,0:T(8,128)S(1)} async-done(((f32[16,20,128]{2,1,0:T(8,128)}), f32[16,20,128]{2,1,0:T(8,128)S(1)}, u32[]{:S(2)}, u32[]{:S(2)}) %all-to-all-start.2) | async-done | bytes 163872 | tf_op jit(solution)/shard_map/all_to_all | solution.py:78
  59.0 0.7 broadcast_in_dim.206
  59.7 7.2 %all-to-all-start.3 = ((bf16[16,18,128]{2,1,0:T(8,128)(2,1)}), bf16[16,18,128]{2,1,0:T(8,128)(2,1)S(1)}, u32[]{:S(2)}, u32[]{:S(2)}) async-start(bf16[16,18,128]{2,1,0:T(8,128)(2,1)} %broadcast_in_dim.206), calls=%async_computation.3 | async-start | bytes 196608 | tf_op jit(solution)/shard_map/all_to_all | solution.py:62
  67.0 0.3 fusion.3
  67.3 11.4 %all-to-all-done.3 = bf16[16,18,128]{2,1,0:T(8,128)(2,1)S(1)} async-done(((bf16[16,18,128]{2,1,0:T(8,128)(2,1)}), bf16[16,18,128]{2,1,0:T(8,128)(2,1)S(1)}, u32[]{:S(2)}, u32[]{:S(2)}) %all-to-all-start.3) | async-done | bytes 73760 | tf_op jit(solution)/shard_map/all_to_all | solution.py:62
  78.9 0.7 broadcast_in_dim.208
  79.6 3.5 %all-to-all-start.4 = ((bf16[4,32,1152]{2,1,0:T(8,128)(2,1)}), bf16[4,32,1152]{2,1,0:T(8,128)(2,1)S(1)}, u32[]{:S(2)}, u32[]{:S(2)}) async-start(bf16[4,32,1152]{2,1,0:T(8,128)(2,1)} %broadcast_in_dim.208), calls=%async_computation.4 | async-start | bytes 589824 | tf_op jit(solution)/shard_map/all_to_all | solution.py:62
  83.1 5.6 %all-to-all-done.4 = bf16[4,32,1152]{2,1,0:T(8,128)(2,1)S(1)} async-done(((bf16[4,32,1152]{2,1,0:T(8,128)(2,1)}), bf16[4,32,1152]{2,1,0:T(8,128)(2,1)S(1)}, u32[]{:S(2)}, u32[]{:S(2)}) %all-to-all-start.4) | async-done | bytes 294944 | tf_op jit(solution)/shard_map/all_to_all | solution.py:62
  88.7 0.2 reshape_reshape.10
  89.1 0.6 gather_fusion.2
  89.8 0.2 copy-done.6
  90.1 0.4 fusion.71
  90.5 0.6 gather_fusion.3
  91.2 0.4 fusion.18
  91.6 0.4 convolution_multiply_fusion.1
  92.0 0.1 convolution_bitcast_fusion
  92.3 0.3 fusion.2
  92.8 0.7 copy-done.2
  93.5 0.5 fusion.72
  94.1 0.4 fusion.16
  94.7 0.4 fusion.14
  95.3 0.5 fusion.8
  95.9 0.3 add_select_fusion
  96.3 9.3 %all_to_all.50 = f32[4,16,16,128]{3,2,1,0:T(8,128)S(1)} all-to-all(f32[4,16,16,128]{3,2,1,0:T(8,128)S(1)} %pad_maximum_fusion), channel_id=1, replica_groups=mesh['kv'=8,'px'=4,'pz'=16] {'px'}, dimensions={0} | all-to-all | bytes 1048576 | tf_op jit(solution)/shard_map/all_to_all | solution.py:253
  105.8 0.2 fusion.7
  106.0 15.3 %all_to_all.51 = f32[16,16,128]{2,1,0:T(8,128)S(1)} all-to-all(f32[16,16,128]{2,1,0:T(8,128)S(1)} %pad_maximum_fusion.2), channel_id=1, replica_groups=mesh['kv'=8,'px'=4,'pz'=16] {'pz'}, dimensions={0} | all-to-all | bytes 262144 | tf_op jit(solution)/shard_map/all_to_all | solution.py:255
  121.6 15.3 %all_to_all.52 = bf16[16,14,128]{2,1,0:T(8,128)(2,1)S(1)} all-to-all(bf16[16,14,128]{2,1,0:T(8,128)(2,1)S(1)} %broadcast_in_dim.222), channel_id=1, replica_groups=mesh['kv'=8,'px'=4,'pz'=16] {'pz'}, dimensions={0} | all-to-all | bytes 114688 | tf_op jit(solution)/shard_map/all_to_all | solution.py:62
  137.0 8.0 %all_to_all.53 = bf16[4,224,128]{2,1,0:T(8,128)(2,1)S(1)} all-to-all(bf16[4,224,128]{2,1,0:T(8,128)(2,1)S(1)} %broadcast_in_dim.224), channel_id=1, replica_groups=mesh['kv'=8,'px'=4,'pz'=16] {'px'}, dimensions={0} | all-to-all | bytes 458752 | tf_op jit(solution)/shard_map/all_to_all | solution.py:62
  145.0 0.2 reshape_reshape.11
  145.3 0.2 convolution_convert_fusion.2
  145.5 18.0 %all_to_all.54 = bf16[8,128,112]{1,2,0:T(8,128)(2,1)S(1)} all-to-all(bf16[8,128,112]{1,2,0:T(8,128)(2,1)S(1)} %broadcast_in_dim.225), channel_id=1, replica_groups=mesh['kv'=8,'px'=4,'pz'=16] {'kv'}, dimensions={0} | all-to-all | bytes 458752 | tf_op jit(solution)/shard_map/all_to_all | solution.py:62
  163.6 0.7 copy.164
  (94 shorter events, 3.3 us)
Async XLA Ops:
  0.6 1.2 copy-start
  1.8 11.5 %copy-start.7 = (s32[8,64]{1,0:T(8,128)S(1)}, s32[8,64]{1,0:T(8,128)}, u32[]{:S(2)}) copy-start(s32[8,64]{1,0:T(8,128)} %param.12) | copy-start | bytes 6148
  1.8 11.9 %copy-start.9 = (bf16[112]{0:T(256)(128)(2,1)S(1)}, bf16[112]{0:T(256)(128)(2,1)}, u32[]{:S(2)}) copy-start(bf16[112]{0:T(256)(128)(2,1)} %param.15) | copy-start | bytes 676
  2.4 17.2 %copy-start.4 = (bf16[112,1152]{1,0:T(8,128)(2,1)S(1)}, bf16[112,1152]{1,0:T(8,128)(2,1)}, u32[]{:S(2)}) copy-start(bf16[112,1152]{1,0:T(8,128)(2,1)} %param.16) | copy-start | bytes 774148
  3.2 16.3 %all-to-all-start = ((bf16[8,128,112]{1,2,0:T(8,128)(2,1)}), bf16[8,128,112]{1,2,0:T(8,128)(2,1)S(1)}, u32[]{:S(2)}, u32[]{:S(2)}) async-start(bf16[8,128,112]{1,2,0:T(8,128)(2,1)} %broadcast_in_dim.203), calls=%async_computation | async-start | bytes 458752 | tf_op jit(solution)/shard_map/all_to_all | solution.py:62
  21.0 3.6 %copy-start.1 = (s32[8]{0:T(128)S(1)}, s32[8]{0:T(128)}, u32[]{:S(2)}) copy-start(s32[8]{0:T(128)} %param.11) | copy-start | bytes 100
  21.0 4.9 %copy-start.8 = (s32[2,64]{1,0:T(2,128)S(1)}, s32[2,64]{1,0:T(2,128)}, u32[]{:S(2)}) copy-start(s32[2,64]{1,0:T(2,128)} %param.13) | copy-start | bytes 1540
  21.0 13.6 %all-to-all-start.1 = ((f32[4,320,128]{2,1,0:T(8,128)}), f32[4,320,128]{2,1,0:T(8,128)S(1)}, u32[]{:S(2)}, u32[]{:S(2)}) async-start(f32[4,320,128]{2,1,0:T(8,128)} %reshape.637), calls=%async_computation.1 | async-start | bytes 1310720 | tf_op jit(solution)/shard_map/all_to_all | solution.py:78
  26.0 41.0 %copy-start.3 = (bf16[2,64,13,128]{3,1,2,0:T(8,128)(2,1)S(1)}, bf16[2,64,13,128]{3,1,2,0:T(8,128)(2,1)}, u32[]{:S(2)}) copy-start(bf16[2,64,13,128]{3,1,2,0:T(8,128)(2,1)} %param.18) | copy-start | bytes 1277956
  35.3 23.3 %all-to-all-start.2 = ((f32[16,20,128]{2,1,0:T(8,128)}), f32[16,20,128]{2,1,0:T(8,128)S(1)}, u32[]{:S(2)}, u32[]{:S(2)}) async-start(f32[16,20,128]{2,1,0:T(8,128)} %reshape_reshape.9), calls=%async_computation.2 | async-start | bytes 393216 | tf_op jit(solution)/shard_map/all_to_all | solution.py:78
  59.7 19.1 %all-to-all-start.3 = ((bf16[16,18,128]{2,1,0:T(8,128)(2,1)}), bf16[16,18,128]{2,1,0:T(8,128)(2,1)S(1)}, u32[]{:S(2)}, u32[]{:S(2)}) async-start(bf16[16,18,128]{2,1,0:T(8,128)(2,1)} %broadcast_in_dim.206), calls=%async_computation.3 | async-start | bytes 196608 | tf_op jit(solution)/shard_map/all_to_all | solution.py:62
  79.6 9.1 %all-to-all-start.4 = ((bf16[4,32,1152]{2,1,0:T(8,128)(2,1)}), bf16[4,32,1152]{2,1,0:T(8,128)(2,1)S(1)}, u32[]{:S(2)}, u32[]{:S(2)}) async-start(bf16[4,32,1152]{2,1,0:T(8,128)(2,1)} %broadcast_in_dim.208), calls=%async_computation.4 | async-start | bytes 589824 | tf_op jit(solution)/shard_map/all_to_all | solution.py:62
  89.0 1.0 copy-start.6
  92.7 0.8 copy-start.2
  121.3 23.9 %copy-start.5 = (bf16[896,112]{0,1:T(8,128)(2,1)S(1)}, bf16[896,112]{0,1:T(8,128)(2,1)}, u32[]{:S(2)}) copy-start(bf16[896,112]{0,1:T(8,128)(2,1)} %param.17) | copy-start | bytes 602116
